TPU v7x, 256 devices: a whole 4x4x8 slice. The times are simulated.
256 devices in a mesh: blk: 32 (over x, y, z_hi), head: 8 (over z_lo, core).
Axes of the slice: x: 4, y: 4, z: 8 (z_hi: 2, z_lo: 4; z = z_hi * 4 + z_lo), core: 2. Of those that a mesh axis runs over, the one named last changes fastest.
Arguments:
- tokens: bfloat16 [16384, 1408], P('blk'), may hold values from -6 to 6
- group_segment: int32 [4096], P('blk'), may hold values from 0 to 15, never falling along the last dimension, each value on 1 to 512 neighbouring positions
- ln1_gain: float32 [1408], replicated, may hold values from 0.1 to 1.9
- ln1_bias: float32 [1408], replicated, may hold values from -3 to 3
- qkv_weight: bfloat16 [1408, 3, 1408], P(None, None, 'head'), may hold values from -1 to 1
- out_weight: bfloat16 [1408, 1408], P('head'), may hold values from -0.15625 to 0.15625
- ln2_gain: float32 [1408], replicated, may hold values from 0.1 to 1.9
- ln2_bias: float32 [1408], replicated, may hold values from -3 to 3
- fc1_weight: bfloat16 [1408, 6144], P(None, 'head'), may hold values from -0.15625 to 0.15625
- fc2_weight: bfloat16 [6144, 1408], P('head'), may hold values from -0.078125 to 0.078125
- proj_weight: bfloat16 [5632, 4096], P('blk', 'head'), may hold values from -0.078125 to 0.078125
Outputs:
- merged_out: bfloat16 [4096, 4096], P('blk', 'head')
- req_rms: float32 [16], replicated
- req_peak: float32 [16], replicated
Inputs may be any that keep to these rules, and one draw needn't show every extreme that they name: `group_segment`: ids never fall along the rows; every request holds 1 to 512 groups, and one holds exactly that many.
All inputs are finite; a program needn't handle non-finite values.
Results may differ from a plain program's by a relative error of at most 0.017.
Values may be sent and summed in bfloat16 or wider, within the bound.
No kernel may reach another device: no remote copies, remote signals or barrier semaphores. Data moves between devices by JAX's collectives and lax.ppermute only.
A program may use at most 64 MiB of HBM per device.

v0:
```python
import jax
import jax.numpy as jnp
from jax import lax
from jax.sharding import PartitionSpec as P

HD = 88
OUTW = 4096
REACH = 4


def passed_along(x, axis, by):
    size = lax.axis_size(axis)
    pairs = [(i, i + by) for i in range(size) if 0 <= i + by < size]
    return lax.ppermute(x, axis, pairs)


def butterfly(summed, peak):
    split = summed.shape[0]
    both = jnp.concatenate([summed, peak])
    for axis in ("head", "blk"):
        size = lax.axis_size(axis)
        if size & (size - 1):
            both = jnp.concatenate(
                [lax.psum(both[:split], axis), lax.pmax(both[split:], axis)]
            )
            continue
        step = 1
        while step < size:
            pairs = [(i, i ^ step) for i in range(size)]
            other = lax.ppermute(both, axis, pairs)
            both = jnp.concatenate(
                [both[:split] + other[:split], jnp.maximum(both[split:], other[split:])]
            )
            step *= 2
    return both[:split], both[split:]


def gather_rows(x, n_head):
    spread = jnp.broadcast_to(x[None], (n_head,) + x.shape)
    got = lax.all_to_all(spread, "head", 0, 0, tiled=True)
    return got.reshape((n_head * x.shape[0],) + x.shape[1:])


def layer_norm(x, gain, bias):
    mean = jnp.mean(x, axis=-1, keepdims=True)
    var = jnp.mean((x - mean) ** 2, axis=-1, keepdims=True)
    return (x - mean) * lax.rsqrt(var + 1e-06) * gain + bias


def per_device(
    tokens,
    group_segment,
    ln1_gain,
    ln1_bias,
    qkv_weight,
    out_weight,
    ln2_gain,
    ln2_bias,
    fc1_weight,
    fc2_weight,
    proj_weight,
):
    rows = tokens.shape[0]
    x_in = tokens.astype(jnp.float32)
    seg_ids = jnp.repeat(group_segment + 1, 4)
    own_low = jnp.min(seg_ids)
    own_high = jnp.max(seg_ids)
    normed = layer_norm(x_in, ln1_gain, ln1_bias).astype(jnp.bfloat16)
    qkv = jnp.einsum("rd,dck->crk", normed, qkv_weight, preferred_element_type=jnp.float32).astype(
        jnp.bfloat16
    )
    local_heads = qkv.shape[2] // HD
    query = qkv[0].reshape(rows, local_heads, HD)
    keys = qkv[1]
    values = qkv[2]
    scale = 1.0 / HD**0.5

    def update(carry, piece):
        top, total, acc = carry
        kpiece, vpiece, ipiece = piece
        count = kpiece.shape[0]
        scores = (
            jnp.einsum(
                "rhe,phe->hrp",
                query,
                kpiece.reshape(count, local_heads, HD),
                preferred_element_type=jnp.float32,
            )
            * scale
        )
        mask = (seg_ids[:, None] == ipiece[None, :])[None]
        new_top = jnp.maximum(top, jnp.max(jnp.where(mask, scores, -1e30), axis=-1))
        factor = jnp.exp(top - new_top)
        weights = jnp.where(mask, jnp.exp(scores - new_top[..., None]), 0.0)
        total = total * factor + jnp.sum(weights, axis=-1)
        acc = acc * factor[..., None] + jnp.einsum(
            "hrp,phe->hre",
            weights.astype(jnp.bfloat16),
            vpiece.reshape(count, local_heads, HD),
            preferred_element_type=jnp.float32,
        )
        return (new_top, total, acc)

    def fold_block(carry, piece):
        ipiece = piece[2]
        touches = (jnp.min(ipiece) <= own_high) & (jnp.max(ipiece) >= own_low)
        return lax.cond(touches, lambda c: update(c, piece), lambda c: c, carry)

    start_state = (
        jnp.full((local_heads, rows), -1e30, jnp.float32),
        jnp.zeros((local_heads, rows), jnp.float32),
        jnp.zeros((local_heads, rows, HD), jnp.float32),
    )
    state = fold_block(start_state, (keys, values, seg_ids))
    width = keys.shape[1]
    packed = jnp.concatenate(
        [keys, values, seg_ids.astype(jnp.bfloat16)[:, None]], axis=1
    )
    packed = jnp.pad(packed, ((0, 0), (0, (-packed.shape[1]) % 128)))
    for distance in range(1, REACH + 1):
        for offset in (distance, -distance):
            got = passed_along(packed, "blk", offset)
            piece = (
                got[:, :width],
                got[:, width : 2 * width],
                got[:, 2 * width].astype(jnp.int32),
            )
            state = fold_block(state, piece)
    top, total, acc = state
    attn = (acc / total[..., None]).astype(jnp.bfloat16)
    attn = jnp.transpose(attn, (1, 0, 2)).reshape(rows, local_heads * HD)
    n_head = lax.axis_size("head")
    share = rows // n_head
    width = x_in.shape[1]
    full_proj_weight = lax.all_gather(proj_weight, "blk", axis=0, tiled=True)
    attn_part = jnp.dot(attn, out_weight, preferred_element_type=jnp.float32).astype(jnp.bfloat16)
    attn_pieces = lax.all_to_all(attn_part.reshape(n_head, share, width), "head", 0, 0, tiled=True)
    x_mine = lax.dynamic_slice_in_dim(x_in, lax.axis_index("head") * share, share, 0)
    h_one = x_mine + jnp.sum(attn_pieces.astype(jnp.float32), axis=0)
    n_two = gather_rows(layer_norm(h_one, ln2_gain, ln2_bias).astype(jnp.bfloat16), n_head)
    hidden = jax.nn.gelu(
        jnp.dot(n_two, fc1_weight, preferred_element_type=jnp.float32), approximate=False
    ).astype(jnp.bfloat16)
    mlp_part = jnp.dot(hidden, fc2_weight, preferred_element_type=jnp.float32).astype(jnp.bfloat16)
    pieces = lax.all_to_all(mlp_part.reshape(n_head, share, width), "head", 0, 0, tiled=True)
    layer_mine = (h_one + jnp.sum(pieces.astype(jnp.float32), axis=0)).astype(jnp.bfloat16)
    layer_mine, full_proj_weight = lax.optimization_barrier((layer_mine, full_proj_weight))
    layer = gather_rows(layer_mine, n_head)
    grouped = layer.reshape(rows // 4, 4 * layer.shape[1])
    proj = jnp.dot(
        grouped,
        full_proj_weight,
        preferred_element_type=jnp.float32,
    )
    requests = lax.axis_size("blk") // 2
    onehot = (group_segment[:, None] == jnp.arange(requests, dtype=jnp.int32)[None, :]).astype(
        jnp.float32
    )
    row_sq = jnp.sum(proj * proj, axis=1)
    local_sq = jnp.dot(row_sq, onehot, precision=lax.Precision.HIGHEST)
    local_count = jnp.sum(onehot, axis=0)
    row_top = jnp.max(jnp.abs(proj), axis=1)
    local_peak = jnp.max(jnp.where(onehot > 0.0, row_top[:, None], 0.0), axis=0)
    summed, req_peak = butterfly(jnp.concatenate([local_sq, local_count]), local_peak)
    tot_sq, tot_count = summed[:requests], summed[requests:]
    counts = tot_count / lax.axis_size("head")
    req_rms = jnp.sqrt(tot_sq / (counts * OUTW) + 1e-06)
    row_rms = jnp.dot(onehot, req_rms, precision=lax.Precision.HIGHEST)
    merged_out = (proj / row_rms[:, None]).astype(jnp.bfloat16)
    return (merged_out, req_rms, req_peak)


def solution(mesh):
    placed = (
        P("blk", None),
        P("blk"),
        P(),
        P(),
        P(None, None, "head"),
        P("head", None),
        P(),
        P(),
        P(None, "head"),
        P("head", None),
        P("blk", "head"),
    )
    return jax.shard_map(
        per_device,
        mesh=mesh,
        in_specs=placed,
        out_specs=(P("blk", "head"), P(), P()),
        check_vma=False,
    )
```

profile of v0, /device:TPU:2, one launch (start us, length us, event | category | flops | bytes accessed | tf_op | source)
XLA Modules:
  0.0 399.9 jit_solution(1209031066453452320)
XLA Ops:
  10.3 2.6 fusion.83
  14.1 9.1 %collective-permute-start.7 = (bf16[512,384]{0,1:T(8,128)(2,1)}, bf16[512,384]{0,1:T(8,128)(2,1)}, u32[]{:S(2)}, u32[]{:S(2)}) collective-permute-start(bf16[512,384]{0,1:T(8,128)(2,1)} %fusion.123), channel_id=1, source_target_pairs={{0,8},{8,16},{16,24},{24,32},{32,40},{40,48},{48,56},{56,64},{64,7... | collective-permute-start | bytes 1179656 | tf_op jit(solution)/shard_map/ppermute | solution.py:14
  23.2 4.3 %collective-permute-start.6 = (bf16[512,384]{0,1:T(8,128)(2,1)}, bf16[512,384]{0,1:T(8,128)(2,1)}, u32[]{:S(2)}, u32[]{:S(2)}) collective-permute-start(bf16[512,384]{0,1:T(8,128)(2,1)} %fusion.123), channel_id=1, source_target_pairs={{8,0},{16,8},{24,16},{32,24},{40,32},{48,40},{56,48},{64,56},{72,6... | collective-permute-start | bytes 1179656 | tf_op jit(solution)/shard_map/ppermute | solution.py:14
  27.6 1.9 collective-permute-start.5
  29.5 6.0 %collective-permute-start.4 = (bf16[512,384]{0,1:T(8,128)(2,1)}, bf16[512,384]{0,1:T(8,128)(2,1)}, u32[]{:S(2)}, u32[]{:S(2)}) collective-permute-start(bf16[512,384]{0,1:T(8,128)(2,1)} %fusion.123), channel_id=1, source_target_pairs={{16,0},{24,8},{32,16},{40,24},{48,32},{56,40},{64,48},{72,56},{80,... | collective-permute-start | bytes 1179656 | tf_op jit(solution)/shard_map/ppermute | solution.py:14
  35.6 4.3 %collective-permute-start.3 = (bf16[512,384]{0,1:T(8,128)(2,1)}, bf16[512,384]{0,1:T(8,128)(2,1)}, u32[]{:S(2)}, u32[]{:S(2)}) collective-permute-start(bf16[512,384]{0,1:T(8,128)(2,1)} %fusion.123), channel_id=1, source_target_pairs={{0,24},{8,32},{16,40},{24,48},{32,56},{40,64},{48,72},{56,80},{64,... | collective-permute-start | bytes 1179656 | tf_op jit(solution)/shard_map/ppermute | solution.py:14
  43.3 4.8 %conditional.9 = (f32[2,512]{1,0:T(2,128)}, f32[2,512]{1,0:T(2,128)S(1)}, f32[2,512,88]{1,2,0:T(8,128)S(1)}) conditional(s32[]{:T(128)} %convert_element_type.182, () %tuple.66, (s32[128,4]{1,0:T(8,128)S(1)}, bf16[1,512,176]{1,2,0:T(8,128)(2,1)S(1)}, bf16[512,2,88]{0,2,1:T(8,128)(2,1)S(1)}, bf16[1,512,176]{1,2,0:T(8,128)(2,1)S(1)}) %tuple.160), branch_computations={%region_20.21_spmd, %region_21.24_spmd} | conditional | flops 190672896 | bytes 8292376 | solution.py:107
  48.1 8.7 %collective-permute-start.2 = (bf16[512,384]{0,1:T(8,128)(2,1)}, bf16[512,384]{0,1:T(8,128)(2,1)}, u32[]{:S(2)}, u32[]{:S(2)}) collective-permute-start(bf16[512,384]{0,1:T(8,128)(2,1)} %fusion.123), channel_id=1, source_target_pairs={{24,0},{32,8},{40,16},{48,24},{56,32},{64,40},{72,48},{80,56},{88,... | collective-permute-start | bytes 1179656 | tf_op jit(solution)/shard_map/ppermute | solution.py:14
  58.2 1.9 collective-permute-start.1
  61.5 6.3 %collective-permute-start = (bf16[512,384]{0,1:T(8,128)(2,1)}, bf16[512,384]{0,1:T(8,128)(2,1)S(1)}, u32[]{:S(2)}, u32[]{:S(2)}) collective-permute-start(bf16[512,384]{0,1:T(8,128)(2,1)} %fusion.123), channel_id=1, source_target_pairs={{32,0},{40,8},{48,16},{56,24},{64,32},{72,40},{80,48},{88,56},{96,... | collective-permute-start | bytes 1179656 | tf_op jit(solution)/shard_map/ppermute | solution.py:14
  84.4 11.9 %collective-permute-done.2 = bf16[512,384]{0,1:T(8,128)(2,1)} collective-permute-done((bf16[512,384]{0,1:T(8,128)(2,1)}, bf16[512,384]{0,1:T(8,128)(2,1)}, u32[]{:S(2)}, u32[]{:S(2)}) %collective-permute-start.2) | collective-permute-done | bytes 393248 | tf_op jit(solution)/shard_map/ppermute | solution.py:14
  109.2 4.2 %conditional.10 = ((f32[2,512]{1,0:T(2,128)}, f32[2,512]{1,0:T(2,128)S(1)}, f32[2,512,88]{1,2,0:T(8,128)S(1)})) conditional(s32[]{:T(128)} %convert_element_type.181, (f32[2,512]{1,0:T(2,128)}, f32[2,512]{1,0:T(2,128)S(1)}, f32[2,512,88]{1,2,0:T(8,128)S(1)}) %conditional.9, (s32[128,4]{1,0:T(8,128)S(1)}, s32[512]{0:T(512)S(1)}, ...), branch_computations={%region_24.25_spmd, %region_25.28_spmd} | conditional | flops 190760960 | bytes 8675360 | solution.py:107
  115.1 4.2 %conditional.11 = ((f32[2,512]{1,0:T(2,128)}, f32[2,512]{1,0:T(2,128)S(1)}, f32[2,512,88]{1,2,0:T(8,128)S(1)})) conditional(s32[]{:T(128)} %convert_element_type.179, (f32[2,512]{1,0:T(2,128)}, f32[2,512]{1,0:T(2,128)S(1)}, f32[2,512,88]{1,2,0:T(8,128)S(1)}) %get-tuple-element.449, (s32[128,4]{1,0:T(8,128)S(1)}, s32[512]{0:T(512)S(1)}, ...), branch_computations={%region_28.29_spmd, %region_29.0_spmd} | conditional | flops 190760960 | bytes 8675360 | solution.py:107
  121.0 4.2 %conditional.12 = ((f32[2,512]{1,0:T(2,128)}, f32[2,512]{1,0:T(2,128)S(1)}, f32[2,512,88]{1,2,0:T(8,128)S(1)})) conditional(s32[]{:T(128)} %convert_element_type.177, (f32[2,512]{1,0:T(2,128)}, f32[2,512]{1,0:T(2,128)S(1)}, f32[2,512,88]{1,2,0:T(8,128)S(1)}) %get-tuple-element.450, (s32[128,4]{1,0:T(8,128)S(1)}, s32[512]{0:T(512)S(1)}, ...), branch_computations={%region_32.33_spmd, %region_33.36_spmd} | conditional | flops 190760960 | bytes 8675360 | solution.py:107
  126.9 4.2 %conditional.13 = ((f32[2,512]{1,0:T(2,128)}, f32[2,512]{1,0:T(2,128)S(1)}, f32[2,512,88]{1,2,0:T(8,128)S(1)})) conditional(s32[]{:T(128)} %convert_element_type.175, (f32[2,512]{1,0:T(2,128)}, f32[2,512]{1,0:T(2,128)S(1)}, f32[2,512,88]{1,2,0:T(8,128)S(1)}) %get-tuple-element.451, (s32[128,4]{1,0:T(8,128)S(1)}, s32[512]{0:T(512)S(1)}, ...), branch_computations={%region_36.37_spmd, %region_37.40_spmd} | conditional | flops 190760960 | bytes 8675360 | solution.py:107
  138.7 11.7 %all-to-all-start = ((bf16[8,64,1408]{2,1,0:T(8,128)(2,1)}), bf16[8,64,1408]{2,1,0:T(8,128)(2,1)}, u32[]{:S(2)}, u32[]{:S(2)}) async-start(bf16[8,64,1408]{2,1,0:T(8,128)(2,1)} %bitcast.95), calls=%async_computation | async-start | bytes 2883584 | tf_op jit(solution)/shard_map/all_to_all | solution.py:137
  150.4 3.1 convert_element_type.160
  153.6 63.4 %all-to-all-done = bf16[8,64,1408]{2,1,0:T(8,128)(2,1)} async-done(((bf16[8,64,1408]{2,1,0:T(8,128)(2,1)}), bf16[8,64,1408]{2,1,0:T(8,128)(2,1)}, u32[]{:S(2)}, u32[]{:S(2)}) %all-to-all-start) | async-done | bytes 1441824 | tf_op jit(solution)/shard_map/all_to_all | solution.py:137
  220.2 38.1 %all_to_all.20 = bf16[8,64,1408]{2,1,0:T(8,128)(2,1)} all-to-all(bf16[8,64,1408]{2,1,0:T(8,128)(2,1)S(1)} %broadcast_in_dim.224), channel_id=1, replica_groups=mesh['blk'=32,'head'=8] {'head'}, dimensions={0} | all-to-all | bytes 2883584 | tf_op jit(solution)/shard_map/all_to_all | solution.py:40
  258.4 9.5 %convolution_convert_fusion = bf16[512,1408]{1,0:T(8,128)(2,1)} fusion(bf16[768,1408]{1,0:T(8,128)(2,1)S(1)} %copy-done, bf16[512,1408]{1,0:T(8,128)(2,1)} %bitcast.96, bf16[1408,768]{1,0:T(8,128)(2,1)} %param.37), kind=kOutput, calls=%fused_computation.118 | convolution fusion | flops 2240872448 | bytes 7208960 | tf_op jit(solution)/shard_map/dot_general | solution.py:144
  267.9 38.5 %all_to_all.21 = bf16[8,64,1408]{2,1,0:T(8,128)(2,1)S(1)} all-to-all(bf16[8,64,1408]{2,1,0:T(8,128)(2,1)} %bitcast.97), channel_id=1, replica_groups=mesh['blk'=32,'head'=8] {'head'}, dimensions={0} | all-to-all | bytes 2883584 | tf_op jit(solution)/shard_map/all_to_all | solution.py:145
  306.7 38.1 %all_to_all.22 = bf16[8,64,1408]{2,1,0:T(8,128)(2,1)} all-to-all(bf16[8,64,1408]{2,1,0:T(8,128)(2,1)S(1)} %broadcast_in_dim.225), channel_id=1, replica_groups=mesh['blk'=32,'head'=8] {'head'}, dimensions={0} | all-to-all | bytes 2883584 | tf_op jit(solution)/shard_map/all_to_all | solution.py:40
  344.8 3.6 reshape_reshape.3
  348.4 4.1 %abs_reduce_fusion = (f32[128]{0:T(128)S(1)}, f32[128]{0:T(128)S(1)}, f32[128,512]{1,0:T(8,128)S(1)}) fusion(bf16[128,5632]{1,0:T(8,128)(2,1)} %reshape_reshape.3, bf16[5632,512]{1,0:T(8,128)(2,1)} %all-gather.2.cloned.1.call-done), kind=kOutput, calls=%fused_computation.194 | convolution fusion | flops 738459392 | bytes 7472128 | tf_op jit(solution)/shard_map/dot_general | solution.py:150
  354.5 3.4 collective-permute-done.9
  358.0 4.5 %collective-permute-done.10 = f32[48]{0:T(128)S(1)} collective-permute-done((f32[48]{0:T(128)S(1)}, f32[48]{0:T(128)S(1)}, u32[]{:S(2)}, u32[]{:S(2)}) %collective-permute-start.10) | collective-permute-done | bytes 224 | tf_op jit(solution)/shard_map/ppermute | solution.py:30
  362.7 4.1 %collective-permute-start.11 = (f32[48]{0:T(128)S(1)}, f32[48]{0:T(128)S(1)}, u32[]{:S(2)}, u32[]{:S(2)}) collective-permute-start(f32[48]{0:T(128)S(1)} %pad_maximum_fusion.3), channel_id=1, source_target_pairs={{0,8},{8,0},{16,24},{24,16},{32,40},{40,32},{48,56},{56,48},{64,72... | collective-permute-start | bytes 584 | tf_op jit(solution)/shard_map/ppermute | solution.py:30
  366.7 3.4 collective-permute-done.11
  371.8 2.1 collective-permute-done.12
  374.0 7.0 %collective-permute-start.13 = (f32[48]{0:T(128)S(1)}, f32[48]{0:T(128)S(1)}, u32[]{:S(2)}, u32[]{:S(2)}) collective-permute-start(f32[48]{0:T(128)S(1)} %pad_maximum_fusion.5), channel_id=1, source_target_pairs={{0,32},{8,40},{16,48},{24,56},{32,0},{40,8},{48,16},{56,24},{64,96... | collective-permute-start | bytes 584 | tf_op jit(solution)/shard_map/ppermute | solution.py:30
  382.8 3.6 collective-permute-done.14
  386.5 5.1 %collective-permute-done.15 = f32[48]{0:T(128)S(1)} collective-permute-done((f32[48]{0:T(128)S(1)}, f32[48]{0:T(128)S(1)}, u32[]{:S(2)}, u32[]{:S(2)}) %collective-permute-start.15) | collective-permute-done | bytes 224 | tf_op jit(solution)/shard_map/ppermute | solution.py:30
  (155 shorter events, 62.2 us)
Async XLA Ops:
  7.2 251.2 %copy-start = (bf16[768,1408]{1,0:T(8,128)(2,1)S(1)}, bf16[768,1408]{1,0:T(8,128)(2,1)}, u32[]{:S(2)}) copy-start(bf16[768,1408]{1,0:T(8,128)(2,1)} %param.38) | copy-start | bytes 6488068
  7.2 3.1 copy-start.8
  7.2 299.4 %all-gather.2.cloned.1.call-start = ((), (), s32[]{:S(2)}) async-start(), calls=%async_computation.4 | async-start | bytes 5947392 | tf_op jit(solution)/shard_map/all_gather | solution.py:135
  7.2 2.5 copy-start.1
  7.2 3.1 copy-start.9
  14.1 34.0 %collective-permute-start.7 = (bf16[512,384]{0,1:T(8,128)(2,1)}, bf16[512,384]{0,1:T(8,128)(2,1)}, u32[]{:S(2)}, u32[]{:S(2)}) collective-permute-start(bf16[512,384]{0,1:T(8,128)(2,1)} %fusion.123), channel_id=1, source_target_pairs={{0,8},{8,16},{16,24},{24,32},{32,40},{40,48},{48,56},{56,64},{64,7... | collective-permute-start | bytes 1179656 | tf_op jit(solution)/shard_map/ppermute | solution.py:14
  23.2 35.0 %collective-permute-start.6 = (bf16[512,384]{0,1:T(8,128)(2,1)}, bf16[512,384]{0,1:T(8,128)(2,1)}, u32[]{:S(2)}, u32[]{:S(2)}) collective-permute-start(bf16[512,384]{0,1:T(8,128)(2,1)} %fusion.123), channel_id=1, source_target_pairs={{8,0},{16,8},{24,16},{32,24},{40,32},{48,40},{56,48},{64,56},{72,6... | collective-permute-start | bytes 1179656 | tf_op jit(solution)/shard_map/ppermute | solution.py:14
  27.6 33.9 %collective-permute-start.5 = (bf16[512,384]{0,1:T(8,128)(2,1)}, bf16[512,384]{0,1:T(8,128)(2,1)}, u32[]{:S(2)}, u32[]{:S(2)}) collective-permute-start(bf16[512,384]{0,1:T(8,128)(2,1)} %fusion.123), channel_id=1, source_target_pairs={{0,16},{8,24},{16,32},{24,40},{32,48},{40,56},{48,64},{56,72},{64,... | collective-permute-start | bytes 1179656 | tf_op jit(solution)/shard_map/ppermute | solution.py:14
  29.5 39.7 %collective-permute-start.4 = (bf16[512,384]{0,1:T(8,128)(2,1)}, bf16[512,384]{0,1:T(8,128)(2,1)}, u32[]{:S(2)}, u32[]{:S(2)}) collective-permute-start(bf16[512,384]{0,1:T(8,128)(2,1)} %fusion.123), channel_id=1, source_target_pairs={{16,0},{24,8},{32,16},{40,24},{48,32},{56,40},{64,48},{72,56},{80,... | collective-permute-start | bytes 1179656 | tf_op jit(solution)/shard_map/ppermute | solution.py:14
  35.6 44.9 %collective-permute-start.3 = (bf16[512,384]{0,1:T(8,128)(2,1)}, bf16[512,384]{0,1:T(8,128)(2,1)}, u32[]{:S(2)}, u32[]{:S(2)}) collective-permute-start(bf16[512,384]{0,1:T(8,128)(2,1)} %fusion.123), channel_id=1, source_target_pairs={{0,24},{8,32},{16,40},{24,48},{32,56},{40,64},{48,72},{56,80},{64,... | collective-permute-start | bytes 1179656 | tf_op jit(solution)/shard_map/ppermute | solution.py:14
  48.1 48.2 %collective-permute-start.2 = (bf16[512,384]{0,1:T(8,128)(2,1)}, bf16[512,384]{0,1:T(8,128)(2,1)}, u32[]{:S(2)}, u32[]{:S(2)}) collective-permute-start(bf16[512,384]{0,1:T(8,128)(2,1)} %fusion.123), channel_id=1, source_target_pairs={{24,0},{32,8},{40,16},{48,24},{56,32},{64,40},{72,48},{80,56},{88,... | collective-permute-start | bytes 1179656 | tf_op jit(solution)/shard_map/ppermute | solution.py:14
  58.2 42.0 %collective-permute-start.1 = (bf16[512,384]{0,1:T(8,128)(2,1)}, bf16[512,384]{0,1:T(8,128)(2,1)}, u32[]{:S(2)}, u32[]{:S(2)}) collective-permute-start(bf16[512,384]{0,1:T(8,128)(2,1)} %fusion.123), channel_id=1, source_target_pairs={{0,32},{8,40},{16,48},{24,56},{32,64},{40,72},{48,80},{56,88},{64,... | collective-permute-start | bytes 1179656 | tf_op jit(solution)/shard_map/ppermute | solution.py:14
  61.5 42.7 %collective-permute-start = (bf16[512,384]{0,1:T(8,128)(2,1)}, bf16[512,384]{0,1:T(8,128)(2,1)S(1)}, u32[]{:S(2)}, u32[]{:S(2)}) collective-permute-start(bf16[512,384]{0,1:T(8,128)(2,1)} %fusion.123), channel_id=1, source_target_pairs={{32,0},{40,8},{48,16},{56,24},{64,32},{72,40},{80,48},{88,56},{96,... | collective-permute-start | bytes 1179656 | tf_op jit(solution)/shard_map/ppermute | solution.py:14
  104.2 3.2 copy-start.3
  136.0 1.0 copy-start.2
  138.7 78.3 %all-to-all-start = ((bf16[8,64,1408]{2,1,0:T(8,128)(2,1)}), bf16[8,64,1408]{2,1,0:T(8,128)(2,1)}, u32[]{:S(2)}, u32[]{:S(2)}) async-start(bf16[8,64,1408]{2,1,0:T(8,128)(2,1)} %bitcast.95), calls=%async_computation | async-start | bytes 2883584 | tf_op jit(solution)/shard_map/all_to_all | solution.py:137
  153.6 66.4 %copy-start.4 = (f32[1408]{0:T(1024)S(1)}, f32[1408]{0:T(1024)}, u32[]{:S(2)}) copy-start(f32[1408]{0:T(1024)} %param.36) | copy-start | bytes 16900
  153.6 66.4 %copy-start.5 = (f32[1408]{0:T(1024)S(1)}, f32[1408]{0:T(1024)}, u32[]{:S(2)}) copy-start(f32[1408]{0:T(1024)} %param.35) | copy-start | bytes 16900
  348.4 4.1 %copy-start.6 = (s32[128]{0:T(128)S(1)}, s32[128]{0:T(128)}, u32[]{:S(2)}) copy-start(s32[128]{0:T(128)} %param.30) | copy-start | bytes 1540
  352.9 1.2 collective-permute-start.8
  354.3 3.6 collective-permute-start.9
  358.0 4.5 %collective-permute-start.10 = (f32[48]{0:T(128)S(1)}, f32[48]{0:T(128)S(1)}, u32[]{:S(2)}, u32[]{:S(2)}) collective-permute-start(f32[48]{0:T(128)S(1)} %pad_maximum_fusion.2), channel_id=1, source_target_pairs={{0,4},{1,5},{2,6},{3,7},{4,0},{5,1},{6,2},{7,3},{8,12},{9,13},{10,... | collective-permute-start | bytes 584 | tf_op jit(solution)/shard_map/ppermute | solution.py:30
  362.7 7.5 %collective-permute-start.11 = (f32[48]{0:T(128)S(1)}, f32[48]{0:T(128)S(1)}, u32[]{:S(2)}, u32[]{:S(2)}) collective-permute-start(f32[48]{0:T(128)S(1)} %pad_maximum_fusion.3), channel_id=1, source_target_pairs={{0,8},{8,0},{16,24},{24,16},{32,40},{40,32},{48,56},{56,48},{64,72... | collective-permute-start | bytes 584 | tf_op jit(solution)/shard_map/ppermute | solution.py:30
  370.3 3.6 collective-permute-start.12
  374.0 8.6 %collective-permute-start.13 = (f32[48]{0:T(128)S(1)}, f32[48]{0:T(128)S(1)}, u32[]{:S(2)}, u32[]{:S(2)}) collective-permute-start(f32[48]{0:T(128)S(1)} %pad_maximum_fusion.5), channel_id=1, source_target_pairs={{0,32},{8,40},{16,48},{24,56},{32,0},{40,8},{48,16},{56,24},{64,96... | collective-permute-start | bytes 584 | tf_op jit(solution)/shard_map/ppermute | solution.py:30
  382.7 3.6 collective-permute-start.14
  386.5 5.1 %collective-permute-start.15 = (f32[48]{0:T(128)S(1)}, f32[48]{0:T(128)S(1)}, u32[]{:S(2)}, u32[]{:S(2)}) collective-permute-start(f32[48]{0:T(128)S(1)} %pad_maximum_fusion.7), channel_id=1, source_target_pairs={{0,128},{8,136},{16,144},{24,152},{32,160},{40,168},{48,176},{56,1... | collective-permute-start | bytes 584 | tf_op jit(solution)/shard_map/ppermute | solution.py:30
  392.2 0.9 copy-start.7
Sparse Core Ops, SparseCore 0:
  40.0 176.1 all-gather.1
where the time goes:
time: 402 us; the launch traced here: 400 us
  blocking collectives  115 us (29%)
  waiting for transfers between devices  100 us (25%)
  starting transfers between devices  67.3 us (17%)
  other arithmetic  40.7 us (10%)
  between operations  37.1 us (9%)
  matrix products  25.5 us (6%)
  local copies, waits for them, and re-layouts  14.3 us (4%)
    all_to_all x2, blocking collectives, gather_rows(): got = lax.all_to_all(spread, 'head', 0, 0, tiled=True)  76.3 us
    all_to_all x1, waiting for transfers between devices, per_device(): lax.all_to_all(attn_part.reshape(n_head, share, width), 'head', 0, 0, til...  63.4 us
    ppermute x8, starting transfers between devices, passed_along(): return lax.ppermute(x, axis, pairs)  42.7 us
    all_to_all x1, blocking collectives, per_device(): lax.all_to_all(mlp_part.reshape(n_head, share, width), 'head', 0, 0, tile...  38.5 us
    ppermute x8, waiting for transfers between devices, butterfly(): other = lax.ppermute(both, axis, pairs)  24.6 us
    ppermute x8, starting transfers between devices, butterfly(): other = lax.ppermute(both, axis, pairs)  12.9 us
    ppermute x8, waiting for transfers between devices, passed_along(): return lax.ppermute(x, axis, pairs)  12 us
    all_to_all x1, starting transfers between devices, per_device(): lax.all_to_all(attn_part.reshape(n_head, share, width), 'head', 0, 0, til...  11.7 us
  transfers between devices with their start and end apart: 18, of which 10 were waited for; matrix products, arithmetic and copies ran while one was open for 15% of the time, Pallas kernels for 0%

commit v1 on v0

--- a/solution.py
+++ b/solution.py
@@ -63,8 +63,6 @@
     rows = tokens.shape[0]
     x_in = tokens.astype(jnp.float32)
     seg_ids = jnp.repeat(group_segment + 1, 4)
-    own_low = jnp.min(seg_ids)
-    own_high = jnp.max(seg_ids)
     normed = layer_norm(x_in, ln1_gain, ln1_bias).astype(jnp.bfloat16)
     qkv = jnp.einsum("rd,dck->crk", normed, qkv_weight, preferred_element_type=jnp.float32).astype(
         jnp.bfloat16
@@ -75,58 +73,34 @@
     values = qkv[2]
     scale = 1.0 / HD**0.5
 
-    def update(carry, piece):
-        top, total, acc = carry
-        kpiece, vpiece, ipiece = piece
-        count = kpiece.shape[0]
-        scores = (
-            jnp.einsum(
-                "rhe,phe->hrp",
-                query,
-                kpiece.reshape(count, local_heads, HD),
-                preferred_element_type=jnp.float32,
-            )
-            * scale
-        )
-        mask = (seg_ids[:, None] == ipiece[None, :])[None]
-        new_top = jnp.maximum(top, jnp.max(jnp.where(mask, scores, -1e30), axis=-1))
-        factor = jnp.exp(top - new_top)
-        weights = jnp.where(mask, jnp.exp(scores - new_top[..., None]), 0.0)
-        total = total * factor + jnp.sum(weights, axis=-1)
-        acc = acc * factor[..., None] + jnp.einsum(
-            "hrp,phe->hre",
-            weights.astype(jnp.bfloat16),
-            vpiece.reshape(count, local_heads, HD),
-            preferred_element_type=jnp.float32,
-        )
-        return (new_top, total, acc)
-
-    def fold_block(carry, piece):
-        ipiece = piece[2]
-        touches = (jnp.min(ipiece) <= own_high) & (jnp.max(ipiece) >= own_low)
-        return lax.cond(touches, lambda c: update(c, piece), lambda c: c, carry)
-
-    start_state = (
-        jnp.full((local_heads, rows), -1e30, jnp.float32),
-        jnp.zeros((local_heads, rows), jnp.float32),
-        jnp.zeros((local_heads, rows, HD), jnp.float32),
-    )
-    state = fold_block(start_state, (keys, values, seg_ids))
     width = keys.shape[1]
     packed = jnp.concatenate(
         [keys, values, seg_ids.astype(jnp.bfloat16)[:, None]], axis=1
     )
     packed = jnp.pad(packed, ((0, 0), (0, (-packed.shape[1]) % 128)))
+    blocks = [packed]
     for distance in range(1, REACH + 1):
         for offset in (distance, -distance):
-            got = passed_along(packed, "blk", offset)
-            piece = (
-                got[:, :width],
-                got[:, width : 2 * width],
-                got[:, 2 * width].astype(jnp.int32),
-            )
-            state = fold_block(state, piece)
-    top, total, acc = state
+            blocks.append(passed_along(packed, "blk", offset))
+    near = jnp.concatenate(blocks, axis=0)
+    count = near.shape[0]
+    near_keys = near[:, :width].reshape(count, local_heads, HD)
+    near_values = near[:, width : 2 * width].reshape(count, local_heads, HD)
+    near_seg = near[:, 2 * width].astype(jnp.int32)
+    mask = (seg_ids[:, None] == near_seg[None, :])[None]
+    scores = (
+        jnp.einsum("rhe,phe->hrp", query, near_keys, preferred_element_type=jnp.float32)
+        * scale
+    )
+    top = jnp.max(jnp.where(mask, scores, -1e30), axis=-1)
+    weights = jnp.where(mask, jnp.exp(scores - top[..., None]), 0.0)
+    total = jnp.sum(weights, axis=-1)
+    acc = jnp.einsum(
+        "hrp,phe->hre",
+        weights.astype(jnp.bfloat16),
+        near_values,
+        preferred_element_type=jnp.float32,
+    )
     attn = (acc / total[..., None]).astype(jnp.bfloat16)
     attn = jnp.transpose(attn, (1, 0, 2)).reshape(rows, local_heads * HD)
     n_head = lax.axis_size("head")

time: 402 us -> 404 us (level)
  waiting for transfers between devices: 100 us -> 125 us
  between operations: 37.1 us -> 14.4 us
  other arithmetic: 40.7 us -> 33.8 us
    ppermute x8, waiting for transfers between devices: 12 us -> 31 us  [passed_along(): return lax.ppermute(x, axis, pairs)]
    sub x0 -> x1, other arithmetic: none -> 18.4 us  [per_device(): weights = jnp.where(mask, jnp.exp(scores - top[..., None]), 0.0)]
    reduce_max x8 -> x0, other arithmetic: 10.1 us -> none  [fold_block(): touches = (jnp.min(ipiece) <= own_high) & (jnp.max(ipiece) >= own_low)]
    all_to_all x1, waiting for transfers between devices: 63.4 us -> 73.4 us  [per_device(): lax.all_to_all(attn_part.reshape(n_head, share, width), 'head', 0, 0, til...]
    unnamed x20 -> x25, local copies, waits for them, and re-layouts: 1.04 us -> 8.87 us
    convert_element_type x9 -> x1, other arithmetic: 5.65 us -> 0.95 us  [per_device(): near_seg = near[:, 2 * width].astype(jnp.int32)]
    slice x7 -> x2, local copies, waits for them, and re-layouts: 6.27 us -> 2.16 us  [the longest x1 2.12 us: per_device(): near_keys = near[:, :width].reshape(count, local_heads, HD)]
    dot_general x10 -> x2, matrix products: 7.37 us -> 10.9 us  [the longest x1 7.92 us: per_device(): jnp.einsum('rhe,phe->hrp', query, near_keys, preferred_element_type=jnp.f...]
  transfers between devices with their start and end apart: 18 -> 18, of which waited for: 10 -> 10; matrix products, arithmetic and copies ran while one was open for 15% -> 16% of each run, Pallas kernels for 0% -> 0%
where the time goes in v1:
time: 404 us; the launch traced here: 403 us
  waiting for transfers between devices  125 us (31%)
  blocking collectives  115 us (28%)
  starting transfers between devices  67.8 us (17%)
  other arithmetic  33.8 us (8%)
  matrix products  29 us (7%)
  local copies, waits for them, and re-layouts  17.5 us (4%)
  between operations  14.4 us (4%)
    all_to_all x2, blocking collectives, gather_rows(): got = lax.all_to_all(spread, 'head', 0, 0, tiled=True)  76.3 us
    all_to_all x1, waiting for transfers between devices, per_device(): lax.all_to_all(attn_part.reshape(n_head, share, width), 'head', 0, 0, til...  73.4 us
    ppermute x8, starting transfers between devices, passed_along(): return lax.ppermute(x, axis, pairs)  42.6 us
    all_to_all x1, blocking collectives, per_device(): lax.all_to_all(mlp_part.reshape(n_head, share, width), 'head', 0, 0, tile...  38.5 us
    ppermute x8, waiting for transfers between devices, passed_along(): return lax.ppermute(x, axis, pairs)  31 us
    ppermute x8, waiting for transfers between devices, butterfly(): other = lax.ppermute(both, axis, pairs)  21 us
    sub x1, other arithmetic, per_device(): weights = jnp.where(mask, jnp.exp(scores - top[..., None]), 0.0)  18.4 us
    ppermute x8, starting transfers between devices, butterfly(): other = lax.ppermute(both, axis, pairs)  13.8 us
  transfers between devices with their start and end apart: 18, of which 10 were waited for; matrix products, arithmetic and copies ran while one was open for 16% of the time, Pallas kernels for 0%

profile of v1, /device:TPU:2, one launch (start us, length us, event | category | flops | bytes accessed | tf_op | source)
XLA Modules:
  0.0 402.6 jit_solution(1623486219145745176)
XLA Ops:
  10.6 2.6 fusion.20
  14.2 9.1 %collective-permute-start = (bf16[512,384]{0,1:T(8,128)(2,1)S(1)}, bf16[512,384]{0,1:T(8,128)(2,1)}, u32[]{:S(2)}, u32[]{:S(2)}) collective-permute-start(bf16[512,384]{0,1:T(8,128)(2,1)S(1)} %get-tuple-element.18), channel_id=1, source_target_pairs={{0,8},{8,16},{16,24},{24,32},{32,40},{40,48},{48,56},{56,64},{64,7... | collective-permute-start | bytes 1179656 | tf_op jit(solution)/shard_map/ppermute | solution.py:14
  23.3 4.3 %collective-permute-start.1 = (bf16[512,384]{0,1:T(8,128)(2,1)S(1)}, bf16[512,384]{0,1:T(8,128)(2,1)}, u32[]{:S(2)}, u32[]{:S(2)}) collective-permute-start(bf16[512,384]{0,1:T(8,128)(2,1)S(1)} %get-tuple-element.18), channel_id=1, source_target_pairs={{8,0},{16,8},{24,16},{32,24},{40,32},{48,40},{56,48},{64,56},{72,6... | collective-permute-start | bytes 1179656 | tf_op jit(solution)/shard_map/ppermute | solution.py:14
  27.7 1.9 collective-permute-start.2
  29.6 6.0 %collective-permute-start.3 = (bf16[512,384]{0,1:T(8,128)(2,1)S(1)}, bf16[512,384]{0,1:T(8,128)(2,1)S(1)}, u32[]{:S(2)}, u32[]{:S(2)}) collective-permute-start(bf16[512,384]{0,1:T(8,128)(2,1)S(1)} %get-tuple-element.18), channel_id=1, source_target_pairs={{16,0},{24,8},{32,16},{40,24},{48,32},{56,40},{64,48},{72,56},{80,... | collective-permute-start | bytes 1179656 | tf_op jit(solution)/shard_map/ppermute | solution.py:14
  35.6 4.3 %collective-permute-start.4 = (bf16[512,384]{0,1:T(8,128)(2,1)S(1)}, bf16[512,384]{0,1:T(8,128)(2,1)S(1)}, u32[]{:S(2)}, u32[]{:S(2)}) collective-permute-start(bf16[512,384]{0,1:T(8,128)(2,1)S(1)} %get-tuple-element.18), channel_id=1, source_target_pairs={{0,24},{8,32},{16,40},{24,48},{32,56},{40,64},{48,72},{56,80},{64,... | collective-permute-start | bytes 1179656 | tf_op jit(solution)/shard_map/ppermute | solution.py:14
  41.6 8.7 %collective-permute-start.5 = (bf16[512,384]{0,1:T(8,128)(2,1)S(1)}, bf16[512,384]{0,1:T(8,128)(2,1)S(1)}, u32[]{:S(2)}, u32[]{:S(2)}) collective-permute-start(bf16[512,384]{0,1:T(8,128)(2,1)S(1)} %get-tuple-element.18), channel_id=1, source_target_pairs={{24,0},{32,8},{40,16},{48,24},{56,32},{64,40},{72,48},{80,56},{88,... | collective-permute-start | bytes 1179656 | tf_op jit(solution)/shard_map/ppermute | solution.py:14
  56.0 6.3 %collective-permute-start.7 = (bf16[512,384]{0,1:T(8,128)(2,1)S(1)}, bf16[512,384]{0,1:T(8,128)(2,1)S(1)}, u32[]{:S(2)}, u32[]{:S(2)}) collective-permute-start(bf16[512,384]{0,1:T(8,128)(2,1)S(1)} %get-tuple-element.18), channel_id=1, source_target_pairs={{32,0},{40,8},{48,16},{56,24},{64,32},{72,40},{80,48},{88,56},{96,... | collective-permute-start | bytes 1179656 | tf_op jit(solution)/shard_map/ppermute | solution.py:14
  65.8 31.0 %collective-permute-done.5 = bf16[512,384]{0,1:T(8,128)(2,1)S(1)} collective-permute-done((bf16[512,384]{0,1:T(8,128)(2,1)S(1)}, bf16[512,384]{0,1:T(8,128)(2,1)S(1)}, u32[]{:S(2)}, u32[]{:S(2)}) %collective-permute-start.5) | collective-permute-done | bytes 393248 | tf_op jit(solution)/shard_map/ppermute | solution.py:14
  99.2 2.1 fusion.109
  102.3 7.9 %fusion.114 = f32[2,512,4608]{2,1,0:T(8,128)} fusion(bf16[512,2,88]{0,2,1:T(8,128)(2,1)S(1)} %bitcast.50, bf16[4608,2,88]{0,2,1:T(8,128)(2,1)S(1)} %bitcast.44), kind=kOutput, calls=%fused_computation.181 | convolution fusion | flops 830472192 | bytes 20676608 | tf_op jit(solution)/shard_map/rhe,phe->hrp/dot_general | solution.py:92
  111.5 18.4 %fusion.111 = (f32[2,512]{1,0:T(2,128)S(1)}, bf16[2,512,4608]{2,1,0:T(8,128)(2,1)S(1)}) fusion(f32[2,512,4608]{2,1,0:T(8,128)} %fusion.114, pred[512,4608]{1,0:T(8,128)(4,1)S(1)} %broadcast_compare_fusion), kind=kOutput, calls=%fused_computation.179 | output fusion | flops 33034752 | bytes 30674944 | tf_op jit(solution)/shard_map/sub | solution.py:96
  130.0 3.0 fusion.31
  134.7 11.3 %all-to-all-start = ((bf16[8,64,1408]{2,1,0:T(8,128)(2,1)}), bf16[8,64,1408]{2,1,0:T(8,128)(2,1)}, u32[]{:S(2)}, u32[]{:S(2)}) async-start(bf16[8,64,1408]{2,1,0:T(8,128)(2,1)} %bitcast.46), calls=%async_computation | async-start | bytes 2883584 | tf_op jit(solution)/shard_map/all_to_all | solution.py:111
  145.9 3.1 convert_element_type.72
  149.0 73.4 %all-to-all-done = bf16[8,64,1408]{2,1,0:T(8,128)(2,1)} async-done(((bf16[8,64,1408]{2,1,0:T(8,128)(2,1)}), bf16[8,64,1408]{2,1,0:T(8,128)(2,1)}, u32[]{:S(2)}, u32[]{:S(2)}) %all-to-all-start) | async-done | bytes 1441824 | tf_op jit(solution)/shard_map/all_to_all | solution.py:111
  225.7 38.1 %all_to_all.20 = bf16[8,64,1408]{2,1,0:T(8,128)(2,1)} all-to-all(bf16[8,64,1408]{2,1,0:T(8,128)(2,1)S(1)} %broadcast_in_dim.41), channel_id=1, replica_groups=mesh['blk'=32,'head'=8] {'head'}, dimensions={0} | all-to-all | bytes 2883584 | tf_op jit(solution)/shard_map/all_to_all | solution.py:40
  263.8 9.4 %convolution_convert_fusion = bf16[512,1408]{1,0:T(8,128)(2,1)} fusion(bf16[768,1408]{1,0:T(8,128)(2,1)S(1)} %copy-done, bf16[512,1408]{1,0:T(8,128)(2,1)} %bitcast.47, bf16[1408,768]{1,0:T(8,128)(2,1)} %param.19), kind=kOutput, calls=%fused_computation.11 | convolution fusion | flops 2240872448 | bytes 7208960 | tf_op jit(solution)/shard_map/dot_general | solution.py:118
  273.2 38.5 %all_to_all.21 = bf16[8,64,1408]{2,1,0:T(8,128)(2,1)S(1)} all-to-all(bf16[8,64,1408]{2,1,0:T(8,128)(2,1)} %bitcast.48), channel_id=1, replica_groups=mesh['blk'=32,'head'=8] {'head'}, dimensions={0} | all-to-all | bytes 2883584 | tf_op jit(solution)/shard_map/all_to_all | solution.py:119
  312.1 38.1 %all_to_all.22 = bf16[8,64,1408]{2,1,0:T(8,128)(2,1)} all-to-all(bf16[8,64,1408]{2,1,0:T(8,128)(2,1)S(1)} %broadcast_in_dim.68), channel_id=1, replica_groups=mesh['blk'=32,'head'=8] {'head'}, dimensions={0} | all-to-all | bytes 2883584 | tf_op jit(solution)/shard_map/all_to_all | solution.py:40
  350.2 3.6 reshape_reshape.3
  353.8 4.1 %abs_reduce_fusion = (f32[128]{0:T(128)S(1)}, f32[128]{0:T(128)S(1)}, f32[128,512]{1,0:T(8,128)S(1)}) fusion(bf16[128,5632]{1,0:T(8,128)(2,1)} %reshape_reshape.3, bf16[5632,512]{1,0:T(8,128)(2,1)} %all-gather.2.cloned.1.call-done), kind=kOutput, calls=%fused_computation.89 | convolution fusion | flops 738459392 | bytes 7472128 | tf_op jit(solution)/shard_map/dot_general | solution.py:124
  359.9 3.4 collective-permute-done.9
  363.5 4.5 %collective-permute-done.10 = f32[48]{0:T(128)S(1)} collective-permute-done((f32[48]{0:T(128)S(1)}, f32[48]{0:T(128)S(1)}, u32[]{:S(2)}, u32[]{:S(2)}) %collective-permute-start.10) | collective-permute-done | bytes 224 | tf_op jit(solution)/shard_map/ppermute | solution.py:30
  368.1 5.3 %collective-permute-start.11 = (f32[48]{0:T(128)S(1)}, f32[48]{0:T(128)S(1)}, u32[]{:S(2)}, u32[]{:S(2)}) collective-permute-start(f32[48]{0:T(128)S(1)} %pad_maximum_fusion.3), channel_id=1, source_target_pairs={{0,8},{8,0},{16,24},{24,16},{32,40},{40,32},{48,56},{56,48},{64,72... | collective-permute-start | bytes 584 | tf_op jit(solution)/shard_map/ppermute | solution.py:30
  373.4 2.2 collective-permute-done.11
  375.7 2.8 collective-permute-start.12
  380.2 2.7 collective-permute-start.13
  383.0 2.4 collective-permute-done.13
  386.0 3.0 collective-permute-done.14
  389.2 2.1 collective-permute-start.15
  391.3 3.0 collective-permute-done.15
  (96 shorter events, 31.6 us)
Async XLA Ops:
  7.2 256.6 %copy-start = (bf16[768,1408]{1,0:T(8,128)(2,1)S(1)}, bf16[768,1408]{1,0:T(8,128)(2,1)}, u32[]{:S(2)}) copy-start(bf16[768,1408]{1,0:T(8,128)(2,1)} %param.20) | copy-start | bytes 6488068
  7.2 3.4 copy-start.7
  7.2 3.4 copy-start.8
  7.2 304.8 %all-gather.2.cloned.1.call-start = ((), (), s32[]{:S(2)}) async-start(), calls=%async_computation.4 | async-start | bytes 5947392 | tf_op jit(solution)/shard_map/all_gather | solution.py:109
  8.3 1.8 copy-start.1
  14.2 27.4 %collective-permute-start = (bf16[512,384]{0,1:T(8,128)(2,1)S(1)}, bf16[512,384]{0,1:T(8,128)(2,1)}, u32[]{:S(2)}, u32[]{:S(2)}) collective-permute-start(bf16[512,384]{0,1:T(8,128)(2,1)S(1)} %get-tuple-element.18), channel_id=1, source_target_pairs={{0,8},{8,16},{16,24},{24,32},{32,40},{40,48},{48,56},{56,64},{64,7... | collective-permute-start | bytes 1179656 | tf_op jit(solution)/shard_map/ppermute | solution.py:14
  23.3 28.9 %collective-permute-start.1 = (bf16[512,384]{0,1:T(8,128)(2,1)S(1)}, bf16[512,384]{0,1:T(8,128)(2,1)}, u32[]{:S(2)}, u32[]{:S(2)}) collective-permute-start(bf16[512,384]{0,1:T(8,128)(2,1)S(1)} %get-tuple-element.18), channel_id=1, source_target_pairs={{8,0},{16,8},{24,16},{32,24},{40,32},{48,40},{56,48},{64,56},{72,6... | collective-permute-start | bytes 1179656 | tf_op jit(solution)/shard_map/ppermute | solution.py:14
  27.7 28.3 %collective-permute-start.2 = (bf16[512,384]{0,1:T(8,128)(2,1)S(1)}, bf16[512,384]{0,1:T(8,128)(2,1)}, u32[]{:S(2)}, u32[]{:S(2)}) collective-permute-start(bf16[512,384]{0,1:T(8,128)(2,1)S(1)} %get-tuple-element.18), channel_id=1, source_target_pairs={{0,16},{8,24},{16,32},{24,40},{32,48},{40,56},{48,64},{56,72},{64,... | collective-permute-start | bytes 1179656 | tf_op jit(solution)/shard_map/ppermute | solution.py:14
  29.6 34.6 %collective-permute-start.3 = (bf16[512,384]{0,1:T(8,128)(2,1)S(1)}, bf16[512,384]{0,1:T(8,128)(2,1)S(1)}, u32[]{:S(2)}, u32[]{:S(2)}) collective-permute-start(bf16[512,384]{0,1:T(8,128)(2,1)S(1)} %get-tuple-element.18), channel_id=1, source_target_pairs={{16,0},{24,8},{32,16},{40,24},{48,32},{56,40},{64,48},{72,56},{80,... | collective-permute-start | bytes 1179656 | tf_op jit(solution)/shard_map/ppermute | solution.py:14
  35.6 29.3 %collective-permute-start.4 = (bf16[512,384]{0,1:T(8,128)(2,1)S(1)}, bf16[512,384]{0,1:T(8,128)(2,1)S(1)}, u32[]{:S(2)}, u32[]{:S(2)}) collective-permute-start(bf16[512,384]{0,1:T(8,128)(2,1)S(1)} %get-tuple-element.18), channel_id=1, source_target_pairs={{0,24},{8,32},{16,40},{24,48},{32,56},{40,64},{48,72},{56,80},{64,... | collective-permute-start | bytes 1179656 | tf_op jit(solution)/shard_map/ppermute | solution.py:14
  41.6 55.1 %collective-permute-start.5 = (bf16[512,384]{0,1:T(8,128)(2,1)S(1)}, bf16[512,384]{0,1:T(8,128)(2,1)S(1)}, u32[]{:S(2)}, u32[]{:S(2)}) collective-permute-start(bf16[512,384]{0,1:T(8,128)(2,1)S(1)} %get-tuple-element.18), channel_id=1, source_target_pairs={{24,0},{32,8},{40,16},{48,24},{56,32},{64,40},{72,48},{80,56},{88,... | collective-permute-start | bytes 1179656 | tf_op jit(solution)/shard_map/ppermute | solution.py:14
  52.2 45.4 %collective-permute-start.6 = (bf16[512,384]{0,1:T(8,128)(2,1)S(1)}, bf16[512,384]{0,1:T(8,128)(2,1)S(1)}, u32[]{:S(2)}, u32[]{:S(2)}) collective-permute-start(bf16[512,384]{0,1:T(8,128)(2,1)S(1)} %get-tuple-element.18), channel_id=1, source_target_pairs={{0,32},{8,40},{16,48},{24,56},{32,64},{40,72},{48,80},{56,88},{64,... | collective-permute-start | bytes 1179656 | tf_op jit(solution)/shard_map/ppermute | solution.py:14
  56.0 42.4 %collective-permute-start.7 = (bf16[512,384]{0,1:T(8,128)(2,1)S(1)}, bf16[512,384]{0,1:T(8,128)(2,1)S(1)}, u32[]{:S(2)}, u32[]{:S(2)}) collective-permute-start(bf16[512,384]{0,1:T(8,128)(2,1)S(1)} %get-tuple-element.18), channel_id=1, source_target_pairs={{32,0},{40,8},{48,16},{56,24},{64,32},{72,40},{80,48},{88,56},{96,... | collective-permute-start | bytes 1179656 | tf_op jit(solution)/shard_map/ppermute | solution.py:14
  129.9 3.0 copy-start.2
  134.7 87.8 %all-to-all-start = ((bf16[8,64,1408]{2,1,0:T(8,128)(2,1)}), bf16[8,64,1408]{2,1,0:T(8,128)(2,1)}, u32[]{:S(2)}, u32[]{:S(2)}) async-start(bf16[8,64,1408]{2,1,0:T(8,128)(2,1)} %bitcast.46), calls=%async_computation | async-start | bytes 2883584 | tf_op jit(solution)/shard_map/all_to_all | solution.py:111
  149.0 76.4 %copy-start.3 = (f32[1408]{0:T(1024)S(1)}, f32[1408]{0:T(1024)}, u32[]{:S(2)}) copy-start(f32[1408]{0:T(1024)} %param.18) | copy-start | bytes 16900
  149.0 76.4 %copy-start.4 = (f32[1408]{0:T(1024)S(1)}, f32[1408]{0:T(1024)}, u32[]{:S(2)}) copy-start(f32[1408]{0:T(1024)} %param.17) | copy-start | bytes 16900
  353.8 4.1 %copy-start.5 = (s32[128]{0:T(128)S(1)}, s32[128]{0:T(128)}, u32[]{:S(2)}) copy-start(s32[128]{0:T(128)} %param.12) | copy-start | bytes 1540
  358.3 1.2 collective-permute-start.8
  359.7 3.6 collective-permute-start.9
  363.4 4.5 %collective-permute-start.10 = (f32[48]{0:T(128)S(1)}, f32[48]{0:T(128)S(1)}, u32[]{:S(2)}, u32[]{:S(2)}) collective-permute-start(f32[48]{0:T(128)S(1)} %pad_maximum_fusion.2), channel_id=1, source_target_pairs={{0,4},{1,5},{2,6},{3,7},{4,0},{5,1},{6,2},{7,3},{8,12},{9,13},{10,... | collective-permute-start | bytes 584 | tf_op jit(solution)/shard_map/ppermute | solution.py:30
  368.1 7.5 %collective-permute-start.11 = (f32[48]{0:T(128)S(1)}, f32[48]{0:T(128)S(1)}, u32[]{:S(2)}, u32[]{:S(2)}) collective-permute-start(f32[48]{0:T(128)S(1)} %pad_maximum_fusion.3), channel_id=1, source_target_pairs={{0,8},{8,0},{16,24},{24,16},{32,40},{40,32},{48,56},{56,48},{64,72... | collective-permute-start | bytes 584 | tf_op jit(solution)/shard_map/ppermute | solution.py:30
  375.7 4.3 %collective-permute-start.12 = (f32[48]{0:T(128)S(1)}, f32[48]{0:T(128)S(1)}, u32[]{:S(2)}, u32[]{:S(2)}) collective-permute-start(f32[48]{0:T(128)S(1)} %pad_maximum_fusion.4), channel_id=1, source_target_pairs={{0,16},{8,24},{16,0},{24,8},{32,48},{40,56},{48,32},{56,40},{64,80... | collective-permute-start | bytes 584 | tf_op jit(solution)/shard_map/ppermute | solution.py:30
  380.2 5.1 %collective-permute-start.13 = (f32[48]{0:T(128)S(1)}, f32[48]{0:T(128)S(1)}, u32[]{:S(2)}, u32[]{:S(2)}) collective-permute-start(f32[48]{0:T(128)S(1)} %pad_maximum_fusion.5), channel_id=1, source_target_pairs={{0,32},{8,40},{16,48},{24,56},{32,0},{40,8},{48,16},{56,24},{64,96... | collective-permute-start | bytes 584 | tf_op jit(solution)/shard_map/ppermute | solution.py:30
  385.5 3.6 collective-permute-start.14
  389.2 5.1 %collective-permute-start.15 = (f32[48]{0:T(128)S(1)}, f32[48]{0:T(128)S(1)}, u32[]{:S(2)}, u32[]{:S(2)}) collective-permute-start(f32[48]{0:T(128)S(1)} %pad_maximum_fusion.7), channel_id=1, source_target_pairs={{0,128},{8,136},{16,144},{24,152},{32,160},{40,168},{48,176},{56,1... | collective-permute-start | bytes 584 | tf_op jit(solution)/shard_map/ppermute | solution.py:30
  394.9 0.9 copy-start.6
Sparse Core Ops, SparseCore 0:
  40.1 182.9 all-gather.1

commit v2 on v1

--- a/solution.py
+++ b/solution.py
@@ -111,6 +111,7 @@
     attn_pieces = lax.all_to_all(attn_part.reshape(n_head, share, width), "head", 0, 0, tiled=True)
     x_mine = lax.dynamic_slice_in_dim(x_in, lax.axis_index("head") * share, share, 0)
     h_one = x_mine + jnp.sum(attn_pieces.astype(jnp.float32), axis=0)
+    h_one, full_proj_weight = lax.optimization_barrier((h_one, full_proj_weight))
     n_two = gather_rows(layer_norm(h_one, ln2_gain, ln2_bias).astype(jnp.bfloat16), n_head)
     hidden = jax.nn.gelu(
         jnp.dot(n_two, fc1_weight, preferred_element_type=jnp.float32), approximate=False
@@ -118,7 +119,6 @@
     mlp_part = jnp.dot(hidden, fc2_weight, preferred_element_type=jnp.float32).astype(jnp.bfloat16)
     pieces = lax.all_to_all(mlp_part.reshape(n_head, share, width), "head", 0, 0, tiled=True)
     layer_mine = (h_one + jnp.sum(pieces.astype(jnp.float32), axis=0)).astype(jnp.bfloat16)
-    layer_mine, full_proj_weight = lax.optimization_barrier((layer_mine, full_proj_weight))
     layer = gather_rows(layer_mine, n_head)
     grouped = layer.reshape(rows // 4, 4 * layer.shape[1])
     proj = jnp.dot(

time: 404 us -> 389 us (0.963)
  waiting for transfers between devices: 125 us -> 80.5 us
  starting transfers between devices: 67.8 us -> 97.7 us
    all_to_all x1, starting transfers between devices: 11.3 us -> 43 us  [per_device(): lax.all_to_all(attn_part.reshape(n_head, share, width), 'head', 0, 0, til...]
    all_to_all x1, waiting for transfers between devices: 73.4 us -> 43.4 us  [per_device(): lax.all_to_all(attn_part.reshape(n_head, share, width), 'head', 0, 0, til...]
    ppermute x8, waiting for transfers between devices: 31 us -> 12.6 us  [passed_along(): return lax.ppermute(x, axis, pairs)]
  transfers between devices with their start and end apart: 18 -> 18, of which waited for: 10 -> 11; matrix products, arithmetic and copies ran while one was open for 16% -> 15% of each run, Pallas kernels for 0% -> 0%
where the time goes in v2:
time: 389 us; the launch traced here: 388 us
  blocking collectives  115 us (30%)
  starting transfers between devices  97.7 us (25%)
  waiting for transfers between devices  80.5 us (21%)
  other arithmetic  33.7 us (9%)
  matrix products  29 us (7%)
  local copies, waits for them, and re-layouts  17.5 us (4%)
  between operations  14.4 us (4%)
    all_to_all x2, blocking collectives, gather_rows(): got = lax.all_to_all(spread, 'head', 0, 0, tiled=True)  76.2 us
    all_to_all x1, waiting for transfers between devices, per_device(): lax.all_to_all(attn_part.reshape(n_head, share, width), 'head', 0, 0, til...  43.4 us
    all_to_all x1, starting transfers between devices, per_device(): lax.all_to_all(attn_part.reshape(n_head, share, width), 'head', 0, 0, til...  43 us
    ppermute x8, starting transfers between devices, passed_along(): return lax.ppermute(x, axis, pairs)  42.7 us
    all_to_all x1, blocking collectives, per_device(): lax.all_to_all(mlp_part.reshape(n_head, share, width), 'head', 0, 0, tile...  38.5 us
    ppermute x8, waiting for transfers between devices, butterfly(): other = lax.ppermute(both, axis, pairs)  23.8 us
    sub x1, other arithmetic, per_device(): weights = jnp.where(mask, jnp.exp(scores - top[..., None]), 0.0)  18.4 us
    ppermute x8, waiting for transfers between devices, passed_along(): return lax.ppermute(x, axis, pairs)  12.6 us
  transfers between devices with their start and end apart: 18, of which 11 were waited for; matrix products, arithmetic and copies ran while one was open for 15% of the time, Pallas kernels for 0%

profile of v2, /device:TPU:2, one launch (start us, length us, event | category | flops | bytes accessed | tf_op | source)
XLA Modules:
  0.0 387.6 jit_solution(12516073329798856320)
XLA Ops:
  11.1 2.6 fusion.20
  14.8 9.1 %collective-permute-start = (bf16[512,384]{0,1:T(8,128)(2,1)S(1)}, bf16[512,384]{0,1:T(8,128)(2,1)}, u32[]{:S(2)}, u32[]{:S(2)}) collective-permute-start(bf16[512,384]{0,1:T(8,128)(2,1)S(1)} %get-tuple-element.16), channel_id=1, source_target_pairs={{0,8},{8,16},{16,24},{24,32},{32,40},{40,48},{48,56},{56,64},{64,7... | collective-permute-start | bytes 1179656 | tf_op jit(solution)/shard_map/ppermute | solution.py:14
  23.8 4.3 %collective-permute-start.1 = (bf16[512,384]{0,1:T(8,128)(2,1)S(1)}, bf16[512,384]{0,1:T(8,128)(2,1)}, u32[]{:S(2)}, u32[]{:S(2)}) collective-permute-start(bf16[512,384]{0,1:T(8,128)(2,1)S(1)} %get-tuple-element.16), channel_id=1, source_target_pairs={{8,0},{16,8},{24,16},{32,24},{40,32},{48,40},{56,48},{64,56},{72,6... | collective-permute-start | bytes 1179656 | tf_op jit(solution)/shard_map/ppermute | solution.py:14
  28.2 1.9 collective-permute-start.2
  30.1 6.0 %collective-permute-start.3 = (bf16[512,384]{0,1:T(8,128)(2,1)S(1)}, bf16[512,384]{0,1:T(8,128)(2,1)S(1)}, u32[]{:S(2)}, u32[]{:S(2)}) collective-permute-start(bf16[512,384]{0,1:T(8,128)(2,1)S(1)} %get-tuple-element.16), channel_id=1, source_target_pairs={{16,0},{24,8},{32,16},{40,24},{48,32},{56,40},{64,48},{72,56},{80,... | collective-permute-start | bytes 1179656 | tf_op jit(solution)/shard_map/ppermute | solution.py:14
  36.2 4.3 %collective-permute-start.4 = (bf16[512,384]{0,1:T(8,128)(2,1)S(1)}, bf16[512,384]{0,1:T(8,128)(2,1)S(1)}, u32[]{:S(2)}, u32[]{:S(2)}) collective-permute-start(bf16[512,384]{0,1:T(8,128)(2,1)S(1)} %get-tuple-element.16), channel_id=1, source_target_pairs={{0,24},{8,32},{16,40},{24,48},{32,56},{40,64},{48,72},{56,80},{64,... | collective-permute-start | bytes 1179656 | tf_op jit(solution)/shard_map/ppermute | solution.py:14
  42.2 8.7 %collective-permute-start.5 = (bf16[512,384]{0,1:T(8,128)(2,1)S(1)}, bf16[512,384]{0,1:T(8,128)(2,1)S(1)}, u32[]{:S(2)}, u32[]{:S(2)}) collective-permute-start(bf16[512,384]{0,1:T(8,128)(2,1)S(1)} %get-tuple-element.16), channel_id=1, source_target_pairs={{24,0},{32,8},{40,16},{48,24},{56,32},{64,40},{72,48},{80,56},{88,... | collective-permute-start | bytes 1179656 | tf_op jit(solution)/shard_map/ppermute | solution.py:14
  52.7 1.9 collective-permute-start.6
  56.5 6.3 %collective-permute-start.7 = (bf16[512,384]{0,1:T(8,128)(2,1)S(1)}, bf16[512,384]{0,1:T(8,128)(2,1)S(1)}, u32[]{:S(2)}, u32[]{:S(2)}) collective-permute-start(bf16[512,384]{0,1:T(8,128)(2,1)S(1)} %get-tuple-element.16), channel_id=1, source_target_pairs={{32,0},{40,8},{48,16},{56,24},{64,32},{72,40},{80,48},{88,56},{96,... | collective-permute-start | bytes 1179656 | tf_op jit(solution)/shard_map/ppermute | solution.py:14
  66.3 8.9 %collective-permute-done.5 = bf16[512,384]{0,1:T(8,128)(2,1)S(1)} collective-permute-done((bf16[512,384]{0,1:T(8,128)(2,1)S(1)}, bf16[512,384]{0,1:T(8,128)(2,1)S(1)}, u32[]{:S(2)}, u32[]{:S(2)}) %collective-permute-start.5) | collective-permute-done | bytes 393248 | tf_op jit(solution)/shard_map/ppermute | solution.py:14
  76.9 3.7 collective-permute-done.7
  82.3 2.1 fusion.108
  84.5 7.9 %fusion.113 = f32[2,512,4608]{2,1,0:T(8,128)} fusion(bf16[512,2,88]{0,2,1:T(8,128)(2,1)S(1)} %bitcast.50, bf16[4608,2,88]{0,2,1:T(8,128)(2,1)S(1)} %bitcast.44), kind=kOutput, calls=%fused_computation.180 | convolution fusion | flops 830472192 | bytes 20676608 | tf_op jit(solution)/shard_map/rhe,phe->hrp/dot_general | solution.py:92
  93.7 18.4 %fusion.110 = (f32[2,512]{1,0:T(2,128)S(1)}, bf16[2,512,4608]{2,1,0:T(8,128)(2,1)S(1)}) fusion(f32[2,512,4608]{2,1,0:T(8,128)} %fusion.113, pred[512,4608]{1,0:T(8,128)(4,1)S(1)} %broadcast_compare_fusion), kind=kOutput, calls=%fused_computation.178 | output fusion | flops 33034752 | bytes 30674944 | tf_op jit(solution)/shard_map/sub | solution.py:96
  112.1 3.0 fusion.31
  116.8 43.0 %all-to-all-start = ((bf16[8,64,1408]{2,1,0:T(8,128)(2,1)}), bf16[8,64,1408]{2,1,0:T(8,128)(2,1)}, u32[]{:S(2)}, u32[]{:S(2)}) async-start(bf16[8,64,1408]{2,1,0:T(8,128)(2,1)} %bitcast.46), calls=%async_computation | async-start | bytes 2883584 | tf_op jit(solution)/shard_map/all_to_all | solution.py:111
  159.8 3.1 convert_element_type.72
  162.9 43.4 %all-to-all-done = bf16[8,64,1408]{2,1,0:T(8,128)(2,1)} async-done(((bf16[8,64,1408]{2,1,0:T(8,128)(2,1)}), bf16[8,64,1408]{2,1,0:T(8,128)(2,1)}, u32[]{:S(2)}, u32[]{:S(2)}) %all-to-all-start) | async-done | bytes 1441824 | tf_op jit(solution)/shard_map/all_to_all | solution.py:111
  209.7 38.1 %all_to_all.20 = bf16[8,64,1408]{2,1,0:T(8,128)(2,1)} all-to-all(bf16[8,64,1408]{2,1,0:T(8,128)(2,1)S(1)} %broadcast_in_dim.41), channel_id=1, replica_groups=mesh['blk'=32,'head'=8] {'head'}, dimensions={0} | all-to-all | bytes 2883584 | tf_op jit(solution)/shard_map/all_to_all | solution.py:40
  247.8 9.4 %convolution_convert_fusion = bf16[512,1408]{1,0:T(8,128)(2,1)} fusion(bf16[768,1408]{1,0:T(8,128)(2,1)S(1)} %copy-done, bf16[512,1408]{1,0:T(8,128)(2,1)} %bitcast.47, bf16[1408,768]{1,0:T(8,128)(2,1)} %param.19), kind=kOutput, calls=%fused_computation.11 | convolution fusion | flops 2240872448 | bytes 7208960 | tf_op jit(solution)/shard_map/dot_general | solution.py:119
  257.2 38.5 %all_to_all.21 = bf16[8,64,1408]{2,1,0:T(8,128)(2,1)S(1)} all-to-all(bf16[8,64,1408]{2,1,0:T(8,128)(2,1)} %bitcast.48), channel_id=1, replica_groups=mesh['blk'=32,'head'=8] {'head'}, dimensions={0} | all-to-all | bytes 2883584 | tf_op jit(solution)/shard_map/all_to_all | solution.py:120
  296.0 38.1 %all_to_all.22 = bf16[8,64,1408]{2,1,0:T(8,128)(2,1)} all-to-all(bf16[8,64,1408]{2,1,0:T(8,128)(2,1)S(1)} %broadcast_in_dim.68), channel_id=1, replica_groups=mesh['blk'=32,'head'=8] {'head'}, dimensions={0} | all-to-all | bytes 2883584 | tf_op jit(solution)/shard_map/all_to_all | solution.py:40
  334.2 3.6 reshape_reshape.3
  337.7 4.1 %abs_reduce_fusion = (f32[128]{0:T(128)S(1)}, f32[128]{0:T(128)S(1)}, f32[128,512]{1,0:T(8,128)S(1)}) fusion(bf16[128,5632]{1,0:T(8,128)(2,1)} %reshape_reshape.3, bf16[5632,512]{1,0:T(8,128)(2,1)} %all-gather.2.cloned.1.call-done), kind=kOutput, calls=%fused_computation.89 | convolution fusion | flops 738459392 | bytes 7472128 | tf_op jit(solution)/shard_map/dot_general | solution.py:124
  343.8 3.4 collective-permute-done.9
  347.4 4.5 %collective-permute-done.10 = f32[48]{0:T(128)S(1)} collective-permute-done((f32[48]{0:T(128)S(1)}, f32[48]{0:T(128)S(1)}, u32[]{:S(2)}, u32[]{:S(2)}) %collective-permute-start.10) | collective-permute-done | bytes 224 | tf_op jit(solution)/shard_map/ppermute | solution.py:30
  352.0 7.7 %collective-permute-start.11 = (f32[48]{0:T(128)S(1)}, f32[48]{0:T(128)S(1)}, u32[]{:S(2)}, u32[]{:S(2)}) collective-permute-start(f32[48]{0:T(128)S(1)} %pad_maximum_fusion.3), channel_id=1, source_target_pairs={{0,8},{8,0},{16,24},{24,16},{32,40},{40,32},{48,56},{56,48},{64,72... | collective-permute-start | bytes 584 | tf_op jit(solution)/shard_map/ppermute | solution.py:30
  362.1 2.9 collective-permute-done.12
  365.2 2.5 collective-permute-start.13
  367.7 2.6 collective-permute-done.13
  370.4 3.6 collective-permute-done.14
  375.0 4.2 %collective-permute-done.15 = f32[48]{0:T(128)S(1)} collective-permute-done((f32[48]{0:T(128)S(1)}, f32[48]{0:T(128)S(1)}, u32[]{:S(2)}, u32[]{:S(2)}) %collective-permute-start.15) | collective-permute-done | bytes 224 | tf_op jit(solution)/shard_map/ppermute | solution.py:30
  (97 shorter events, 31.2 us)
Async XLA Ops:
  7.2 240.6 %copy-start = (bf16[768,1408]{1,0:T(8,128)(2,1)S(1)}, bf16[768,1408]{1,0:T(8,128)(2,1)}, u32[]{:S(2)}) copy-start(bf16[768,1408]{1,0:T(8,128)(2,1)} %param.20) | copy-start | bytes 6488068
  7.2 3.9 %copy-start.7 = (f32[1408]{0:T(1024)S(1)}, f32[1408]{0:T(1024)}, u32[]{:S(2)}) copy-start(f32[1408]{0:T(1024)} %param.14) | copy-start | bytes 16900
  7.2 3.9 %copy-start.8 = (f32[1408]{0:T(1024)S(1)}, f32[1408]{0:T(1024)}, u32[]{:S(2)}) copy-start(f32[1408]{0:T(1024)} %param.13) | copy-start | bytes 16900
  7.2 201.8 %all-gather.2.cloned.1.call-start = ((), (), s32[]{:S(2)}) async-start(), calls=%async_computation.4 | async-start | bytes 5947392 | tf_op jit(solution)/shard_map/all_gather | solution.py:109
  8.8 1.8 copy-start.1
  14.8 27.4 %collective-permute-start = (bf16[512,384]{0,1:T(8,128)(2,1)S(1)}, bf16[512,384]{0,1:T(8,128)(2,1)}, u32[]{:S(2)}, u32[]{:S(2)}) collective-permute-start(bf16[512,384]{0,1:T(8,128)(2,1)S(1)} %get-tuple-element.16), channel_id=1, source_target_pairs={{0,8},{8,16},{16,24},{24,32},{32,40},{40,48},{48,56},{56,64},{64,7... | collective-permute-start | bytes 1179656 | tf_op jit(solution)/shard_map/ppermute | solution.py:14
  23.8 28.9 %collective-permute-start.1 = (bf16[512,384]{0,1:T(8,128)(2,1)S(1)}, bf16[512,384]{0,1:T(8,128)(2,1)}, u32[]{:S(2)}, u32[]{:S(2)}) collective-permute-start(bf16[512,384]{0,1:T(8,128)(2,1)S(1)} %get-tuple-element.16), channel_id=1, source_target_pairs={{8,0},{16,8},{24,16},{32,24},{40,32},{48,40},{56,48},{64,56},{72,6... | collective-permute-start | bytes 1179656 | tf_op jit(solution)/shard_map/ppermute | solution.py:14
  28.2 28.3 %collective-permute-start.2 = (bf16[512,384]{0,1:T(8,128)(2,1)S(1)}, bf16[512,384]{0,1:T(8,128)(2,1)}, u32[]{:S(2)}, u32[]{:S(2)}) collective-permute-start(bf16[512,384]{0,1:T(8,128)(2,1)S(1)} %get-tuple-element.16), channel_id=1, source_target_pairs={{0,16},{8,24},{16,32},{24,40},{32,48},{40,56},{48,64},{56,72},{64,... | collective-permute-start | bytes 1179656 | tf_op jit(solution)/shard_map/ppermute | solution.py:14
  30.1 34.5 %collective-permute-start.3 = (bf16[512,384]{0,1:T(8,128)(2,1)S(1)}, bf16[512,384]{0,1:T(8,128)(2,1)S(1)}, u32[]{:S(2)}, u32[]{:S(2)}) collective-permute-start(bf16[512,384]{0,1:T(8,128)(2,1)S(1)} %get-tuple-element.16), channel_id=1, source_target_pairs={{16,0},{24,8},{32,16},{40,24},{48,32},{56,40},{64,48},{72,56},{80,... | collective-permute-start | bytes 1179656 | tf_op jit(solution)/shard_map/ppermute | solution.py:14
  36.2 29.3 %collective-permute-start.4 = (bf16[512,384]{0,1:T(8,128)(2,1)S(1)}, bf16[512,384]{0,1:T(8,128)(2,1)S(1)}, u32[]{:S(2)}, u32[]{:S(2)}) collective-permute-start(bf16[512,384]{0,1:T(8,128)(2,1)S(1)} %get-tuple-element.16), channel_id=1, source_target_pairs={{0,24},{8,32},{16,40},{24,48},{32,56},{40,64},{48,72},{56,80},{64,... | collective-permute-start | bytes 1179656 | tf_op jit(solution)/shard_map/ppermute | solution.py:14
  42.2 33.1 %collective-permute-start.5 = (bf16[512,384]{0,1:T(8,128)(2,1)S(1)}, bf16[512,384]{0,1:T(8,128)(2,1)S(1)}, u32[]{:S(2)}, u32[]{:S(2)}) collective-permute-start(bf16[512,384]{0,1:T(8,128)(2,1)S(1)} %get-tuple-element.16), channel_id=1, source_target_pairs={{24,0},{32,8},{40,16},{48,24},{56,32},{64,40},{72,48},{80,56},{88,... | collective-permute-start | bytes 1179656 | tf_op jit(solution)/shard_map/ppermute | solution.py:14
  52.7 23.3 %collective-permute-start.6 = (bf16[512,384]{0,1:T(8,128)(2,1)S(1)}, bf16[512,384]{0,1:T(8,128)(2,1)S(1)}, u32[]{:S(2)}, u32[]{:S(2)}) collective-permute-start(bf16[512,384]{0,1:T(8,128)(2,1)S(1)} %get-tuple-element.16), channel_id=1, source_target_pairs={{0,32},{8,40},{16,48},{24,56},{32,64},{40,72},{48,80},{56,88},{64,... | collective-permute-start | bytes 1179656 | tf_op jit(solution)/shard_map/ppermute | solution.py:14
  56.5 24.1 %collective-permute-start.7 = (bf16[512,384]{0,1:T(8,128)(2,1)S(1)}, bf16[512,384]{0,1:T(8,128)(2,1)S(1)}, u32[]{:S(2)}, u32[]{:S(2)}) collective-permute-start(bf16[512,384]{0,1:T(8,128)(2,1)S(1)} %get-tuple-element.16), channel_id=1, source_target_pairs={{32,0},{40,8},{48,16},{56,24},{64,32},{72,40},{80,48},{88,56},{96,... | collective-permute-start | bytes 1179656 | tf_op jit(solution)/shard_map/ppermute | solution.py:14
  112.1 3.0 copy-start.2
  116.8 89.5 %all-to-all-start = ((bf16[8,64,1408]{2,1,0:T(8,128)(2,1)}), bf16[8,64,1408]{2,1,0:T(8,128)(2,1)}, u32[]{:S(2)}, u32[]{:S(2)}) async-start(bf16[8,64,1408]{2,1,0:T(8,128)(2,1)} %bitcast.46), calls=%async_computation | async-start | bytes 2883584 | tf_op jit(solution)/shard_map/all_to_all | solution.py:111
  162.9 46.4 %copy-start.3 = (f32[1408]{0:T(1024)S(1)}, f32[1408]{0:T(1024)}, u32[]{:S(2)}) copy-start(f32[1408]{0:T(1024)} %param.18) | copy-start | bytes 16900
  162.9 46.5 %copy-start.4 = (f32[1408]{0:T(1024)S(1)}, f32[1408]{0:T(1024)}, u32[]{:S(2)}) copy-start(f32[1408]{0:T(1024)} %param.17) | copy-start | bytes 16900
  337.7 4.1 %copy-start.5 = (s32[128]{0:T(128)S(1)}, s32[128]{0:T(128)}, u32[]{:S(2)}) copy-start(s32[128]{0:T(128)} %param.12) | copy-start | bytes 1540
  342.2 1.2 collective-permute-start.8
  343.6 3.6 collective-permute-start.9
  347.3 4.5 %collective-permute-start.10 = (f32[48]{0:T(128)S(1)}, f32[48]{0:T(128)S(1)}, u32[]{:S(2)}, u32[]{:S(2)}) collective-permute-start(f32[48]{0:T(128)S(1)} %pad_maximum_fusion.2), channel_id=1, source_target_pairs={{0,4},{1,5},{2,6},{3,7},{4,0},{5,1},{6,2},{7,3},{8,12},{9,13},{10,... | collective-permute-start | bytes 584 | tf_op jit(solution)/shard_map/ppermute | solution.py:30
  352.0 9.3 %collective-permute-start.11 = (f32[48]{0:T(128)S(1)}, f32[48]{0:T(128)S(1)}, u32[]{:S(2)}, u32[]{:S(2)}) collective-permute-start(f32[48]{0:T(128)S(1)} %pad_maximum_fusion.3), channel_id=1, source_target_pairs={{0,8},{8,0},{16,24},{24,16},{32,40},{40,32},{48,56},{56,48},{64,72... | collective-permute-start | bytes 584 | tf_op jit(solution)/shard_map/ppermute | solution.py:30
  361.4 3.6 collective-permute-start.12
  365.2 5.1 %collective-permute-start.13 = (f32[48]{0:T(128)S(1)}, f32[48]{0:T(128)S(1)}, u32[]{:S(2)}, u32[]{:S(2)}) collective-permute-start(f32[48]{0:T(128)S(1)} %pad_maximum_fusion.5), channel_id=1, source_target_pairs={{0,32},{8,40},{16,48},{24,56},{32,0},{40,8},{48,16},{56,24},{64,96... | collective-permute-start | bytes 584 | tf_op jit(solution)/shard_map/ppermute | solution.py:30
  370.4 3.6 collective-permute-start.14
  374.1 5.1 %collective-permute-start.15 = (f32[48]{0:T(128)S(1)}, f32[48]{0:T(128)S(1)}, u32[]{:S(2)}, u32[]{:S(2)}) collective-permute-start(f32[48]{0:T(128)S(1)} %pad_maximum_fusion.7), channel_id=1, source_target_pairs={{0,128},{8,136},{16,144},{24,152},{32,160},{40,168},{48,176},{56,1... | collective-permute-start | bytes 584 | tf_op jit(solution)/shard_map/ppermute | solution.py:30
  379.8 0.9 copy-start.6
Sparse Core Ops, SparseCore 0:
  11.4 174.9 all-gather.1

commit v3 on v2

--- a/solution.py
+++ b/solution.py
@@ -77,7 +77,6 @@
     packed = jnp.concatenate(
         [keys, values, seg_ids.astype(jnp.bfloat16)[:, None]], axis=1
     )
-    packed = jnp.pad(packed, ((0, 0), (0, (-packed.shape[1]) % 128)))
     blocks = [packed]
     for distance in range(1, REACH + 1):
         for offset in (distance, -distance):

time: 389 us -> 387 us (level)
  waiting for transfers between devices: 80.5 us -> 113 us
  starting transfers between devices: 97.7 us -> 65.4 us
    all_to_all x1, starting transfers between devices: 43 us -> 9.89 us  [per_device(): lax.all_to_all(attn_part.reshape(n_head, share, width), 'head', 0, 0, til...]
    ppermute x8, waiting for transfers between devices: 12.6 us -> 32.2 us  [passed_along(): return lax.ppermute(x, axis, pairs)]
    all_to_all x1, waiting for transfers between devices: 43.4 us -> 59.2 us  [per_device(): lax.all_to_all(attn_part.reshape(n_head, share, width), 'head', 0, 0, til...]
  transfers between devices with their start and end apart: 18 -> 18, of which waited for: 11 -> 10; matrix products, arithmetic and copies ran while one was open for 15% -> 15% of each run, Pallas kernels for 0% -> 0%
where the time goes in v3:
time: 387 us; the launch traced here: 386 us
  blocking collectives  115 us (30%)
  waiting for transfers between devices  113 us (29%)
  starting transfers between devices  65.4 us (17%)
  other arithmetic  33.1 us (9%)
  matrix products  29.1 us (8%)
  local copies, waits for them, and re-layouts  15.9 us (4%)
  between operations  14.4 us (4%)
    all_to_all x2, blocking collectives, gather_rows(): got = lax.all_to_all(spread, 'head', 0, 0, tiled=True)  76.2 us
    all_to_all x1, waiting for transfers between devices, per_device(): lax.all_to_all(attn_part.reshape(n_head, share, width), 'head', 0, 0, til...  59.2 us
    ppermute x8, starting transfers between devices, passed_along(): return lax.ppermute(x, axis, pairs)  42.7 us
    all_to_all x1, blocking collectives, per_device(): lax.all_to_all(mlp_part.reshape(n_head, share, width), 'head', 0, 0, tile...  38.5 us
    ppermute x8, waiting for transfers between devices, passed_along(): return lax.ppermute(x, axis, pairs)  32.2 us
    ppermute x8, waiting for transfers between devices, butterfly(): other = lax.ppermute(both, axis, pairs)  21.3 us
    sub x1, other arithmetic, per_device(): weights = jnp.where(mask, jnp.exp(scores - top[..., None]), 0.0)  18.4 us
    ppermute x8, starting transfers between devices, butterfly(): other = lax.ppermute(both, axis, pairs)  12.8 us
  transfers between devices with their start and end apart: 18, of which 10 were waited for; matrix products, arithmetic and copies ran while one was open for 15% of the time, Pallas kernels for 0%

profile of v3, /device:TPU:2, one launch (start us, length us, event | category | flops | bytes accessed | tf_op | source)
XLA Modules:
  0.0 386.0 jit_solution(9238932891228674695)
XLA Ops:
  10.3 2.6 fusion.20
  14.1 9.1 %collective-permute-start = (bf16[512,353]{0,1:T(8,128)(2,1)S(1)}, bf16[512,353]{0,1:T(8,128)(2,1)}, u32[]{:S(2)}, u32[]{:S(2)}) collective-permute-start(bf16[512,353]{0,1:T(8,128)(2,1)S(1)} %get-tuple-element.16), channel_id=1, source_target_pairs={{0,8},{8,16},{16,24},{24,32},{32,40},{40,48},{48,56},{56,64},{64,7... | collective-permute-start | bytes 1084424 | tf_op jit(solution)/shard_map/ppermute | solution.py:14
  23.2 4.3 %collective-permute-start.1 = (bf16[512,353]{0,1:T(8,128)(2,1)S(1)}, bf16[512,353]{0,1:T(8,128)(2,1)}, u32[]{:S(2)}, u32[]{:S(2)}) collective-permute-start(bf16[512,353]{0,1:T(8,128)(2,1)S(1)} %get-tuple-element.16), channel_id=1, source_target_pairs={{8,0},{16,8},{24,16},{32,24},{40,32},{48,40},{56,48},{64,56},{72,6... | collective-permute-start | bytes 1084424 | tf_op jit(solution)/shard_map/ppermute | solution.py:14
  27.5 1.9 collective-permute-start.2
  29.5 6.0 %collective-permute-start.3 = (bf16[512,353]{0,1:T(8,128)(2,1)S(1)}, bf16[512,353]{0,1:T(8,128)(2,1)S(1)}, u32[]{:S(2)}, u32[]{:S(2)}) collective-permute-start(bf16[512,353]{0,1:T(8,128)(2,1)S(1)} %get-tuple-element.16), channel_id=1, source_target_pairs={{16,0},{24,8},{32,16},{40,24},{48,32},{56,40},{64,48},{72,56},{80,... | collective-permute-start | bytes 1084424 | tf_op jit(solution)/shard_map/ppermute | solution.py:14
  35.5 4.3 %collective-permute-start.4 = (bf16[512,353]{0,1:T(8,128)(2,1)S(1)}, bf16[512,353]{0,1:T(8,128)(2,1)S(1)}, u32[]{:S(2)}, u32[]{:S(2)}) collective-permute-start(bf16[512,353]{0,1:T(8,128)(2,1)S(1)} %get-tuple-element.16), channel_id=1, source_target_pairs={{0,24},{8,32},{16,40},{24,48},{32,56},{40,64},{48,72},{56,80},{64,... | collective-permute-start | bytes 1084424 | tf_op jit(solution)/shard_map/ppermute | solution.py:14
  40.0 8.7 %collective-permute-start.5 = (bf16[512,353]{0,1:T(8,128)(2,1)S(1)}, bf16[512,353]{0,1:T(8,128)(2,1)S(1)}, u32[]{:S(2)}, u32[]{:S(2)}) collective-permute-start(bf16[512,353]{0,1:T(8,128)(2,1)S(1)} %get-tuple-element.16), channel_id=1, source_target_pairs={{24,0},{32,8},{40,16},{48,24},{56,32},{64,40},{72,48},{80,56},{88,... | collective-permute-start | bytes 1084424 | tf_op jit(solution)/shard_map/ppermute | solution.py:14
  54.3 6.3 %collective-permute-start.7 = (bf16[512,353]{0,1:T(8,128)(2,1)S(1)}, bf16[512,353]{0,1:T(8,128)(2,1)S(1)}, u32[]{:S(2)}, u32[]{:S(2)}) collective-permute-start(bf16[512,353]{0,1:T(8,128)(2,1)S(1)} %get-tuple-element.16), channel_id=1, source_target_pairs={{32,0},{40,8},{48,16},{56,24},{64,32},{72,40},{80,48},{88,56},{96,... | collective-permute-start | bytes 1084424 | tf_op jit(solution)/shard_map/ppermute | solution.py:14
  64.1 32.1 %collective-permute-done.5 = bf16[512,353]{0,1:T(8,128)(2,1)S(1)} collective-permute-done((bf16[512,353]{0,1:T(8,128)(2,1)S(1)}, bf16[512,353]{0,1:T(8,128)(2,1)S(1)}, u32[]{:S(2)}, u32[]{:S(2)}) %collective-permute-start.5) | collective-permute-done | bytes 361504 | tf_op jit(solution)/shard_map/ppermute | solution.py:14
  99.6 2.1 fusion.103
  101.7 8.1 %fusion.108 = f32[2,512,4608]{2,1,0:T(8,128)} fusion(bf16[512,2,88]{0,2,1:T(8,128)(2,1)S(1)} %bitcast.50, bf16[4608,2,88]{0,2,1:T(8,128)(2,1)S(1)} %bitcast.44), kind=kOutput, calls=%fused_computation.175 | convolution fusion | flops 830472192 | bytes 20676608 | tf_op jit(solution)/shard_map/rhe,phe->hrp/dot_general | solution.py:91
  111.1 18.4 %fusion.105 = (f32[2,512]{1,0:T(2,128)S(1)}, bf16[2,512,4608]{2,1,0:T(8,128)(2,1)S(1)}) fusion(f32[2,512,4608]{2,1,0:T(8,128)} %fusion.108, pred[512,4608]{1,0:T(8,128)(4,1)S(1)} %broadcast_compare_fusion), kind=kOutput, calls=%fused_computation.173 | output fusion | flops 33034752 | bytes 30674944 | tf_op jit(solution)/shard_map/sub | solution.py:95
  129.5 3.0 fusion.31
  134.2 9.9 %all-to-all-start = ((bf16[8,64,1408]{2,1,0:T(8,128)(2,1)}), bf16[8,64,1408]{2,1,0:T(8,128)(2,1)}, u32[]{:S(2)}, u32[]{:S(2)}) async-start(bf16[8,64,1408]{2,1,0:T(8,128)(2,1)} %bitcast.46), calls=%async_computation | async-start | bytes 2883584 | tf_op jit(solution)/shard_map/all_to_all | solution.py:110
  144.1 3.2 convert_element_type.70
  147.3 59.2 %all-to-all-done = bf16[8,64,1408]{2,1,0:T(8,128)(2,1)} async-done(((bf16[8,64,1408]{2,1,0:T(8,128)(2,1)}), bf16[8,64,1408]{2,1,0:T(8,128)(2,1)}, u32[]{:S(2)}, u32[]{:S(2)}) %all-to-all-start) | async-done | bytes 1441824 | tf_op jit(solution)/shard_map/all_to_all | solution.py:110
  209.9 38.1 %all_to_all.20 = bf16[8,64,1408]{2,1,0:T(8,128)(2,1)} all-to-all(bf16[8,64,1408]{2,1,0:T(8,128)(2,1)S(1)} %broadcast_in_dim.41), channel_id=1, replica_groups=mesh['blk'=32,'head'=8] {'head'}, dimensions={0} | all-to-all | bytes 2883584 | tf_op jit(solution)/shard_map/all_to_all | solution.py:40
  248.0 9.4 %convolution_convert_fusion = bf16[512,1408]{1,0:T(8,128)(2,1)} fusion(bf16[768,1408]{1,0:T(8,128)(2,1)S(1)} %copy-done, bf16[512,1408]{1,0:T(8,128)(2,1)} %bitcast.47, bf16[1408,768]{1,0:T(8,128)(2,1)} %param.19), kind=kOutput, calls=%fused_computation.11 | convolution fusion | flops 2240872448 | bytes 7208960 | tf_op jit(solution)/shard_map/dot_general | solution.py:118
  257.4 38.5 %all_to_all.21 = bf16[8,64,1408]{2,1,0:T(8,128)(2,1)S(1)} all-to-all(bf16[8,64,1408]{2,1,0:T(8,128)(2,1)} %bitcast.48), channel_id=1, replica_groups=mesh['blk'=32,'head'=8] {'head'}, dimensions={0} | all-to-all | bytes 2883584 | tf_op jit(solution)/shard_map/all_to_all | solution.py:119
  296.2 38.1 %all_to_all.22 = bf16[8,64,1408]{2,1,0:T(8,128)(2,1)} all-to-all(bf16[8,64,1408]{2,1,0:T(8,128)(2,1)S(1)} %broadcast_in_dim.68), channel_id=1, replica_groups=mesh['blk'=32,'head'=8] {'head'}, dimensions={0} | all-to-all | bytes 2883584 | tf_op jit(solution)/shard_map/all_to_all | solution.py:40
  334.4 3.6 reshape_reshape.3
  337.9 4.1 %abs_reduce_fusion = (f32[128]{0:T(128)S(1)}, f32[128]{0:T(128)S(1)}, f32[128,512]{1,0:T(8,128)S(1)}) fusion(bf16[128,5632]{1,0:T(8,128)(2,1)} %reshape_reshape.3, bf16[5632,512]{1,0:T(8,128)(2,1)} %all-gather.2.cloned.1.call-done), kind=kOutput, calls=%fused_computation.84 | convolution fusion | flops 738459392 | bytes 7472128 | tf_op jit(solution)/shard_map/dot_general | solution.py:123
  344.0 3.4 collective-permute-done.9
  347.6 4.5 %collective-permute-done.10 = f32[48]{0:T(128)S(1)} collective-permute-done((f32[48]{0:T(128)S(1)}, f32[48]{0:T(128)S(1)}, u32[]{:S(2)}, u32[]{:S(2)}) %collective-permute-start.10) | collective-permute-done | bytes 224 | tf_op jit(solution)/shard_map/ppermute | solution.py:30
  352.2 5.3 %collective-permute-start.11 = (f32[48]{0:T(128)S(1)}, f32[48]{0:T(128)S(1)}, u32[]{:S(2)}, u32[]{:S(2)}) collective-permute-start(f32[48]{0:T(128)S(1)} %pad_maximum_fusion.4), channel_id=1, source_target_pairs={{0,8},{8,0},{16,24},{24,16},{32,40},{40,32},{48,56},{56,48},{64,72... | collective-permute-start | bytes 584 | tf_op jit(solution)/shard_map/ppermute | solution.py:30
  357.5 2.2 collective-permute-done.11
  361.3 2.1 collective-permute-done.12
  363.6 3.0 collective-permute-start.13
  366.6 2.1 collective-permute-done.13
  369.4 3.0 collective-permute-done.14
  372.5 2.1 collective-permute-start.15
  374.6 3.0 collective-permute-done.15
  (97 shorter events, 29.9 us)
Async XLA Ops:
  7.2 240.8 %copy-start = (bf16[768,1408]{1,0:T(8,128)(2,1)S(1)}, bf16[768,1408]{1,0:T(8,128)(2,1)}, u32[]{:S(2)}) copy-start(bf16[768,1408]{1,0:T(8,128)(2,1)} %param.20) | copy-start | bytes 6488068
  7.2 3.1 copy-start.7
  7.2 3.1 copy-start.8
  7.2 202.0 %all-gather.2.cloned.1.call-start = ((), (), s32[]{:S(2)}) async-start(), calls=%async_computation.4 | async-start | bytes 5947392 | tf_op jit(solution)/shard_map/all_gather | solution.py:108
  7.9 1.8 copy-start.1
  10.3 2.6 copy-start.5
  14.1 25.9 %collective-permute-start = (bf16[512,353]{0,1:T(8,128)(2,1)S(1)}, bf16[512,353]{0,1:T(8,128)(2,1)}, u32[]{:S(2)}, u32[]{:S(2)}) collective-permute-start(bf16[512,353]{0,1:T(8,128)(2,1)S(1)} %get-tuple-element.16), channel_id=1, source_target_pairs={{0,8},{8,16},{16,24},{24,32},{32,40},{40,48},{48,56},{56,64},{64,7... | collective-permute-start | bytes 1084424 | tf_op jit(solution)/shard_map/ppermute | solution.py:14
  23.2 27.4 %collective-permute-start.1 = (bf16[512,353]{0,1:T(8,128)(2,1)S(1)}, bf16[512,353]{0,1:T(8,128)(2,1)}, u32[]{:S(2)}, u32[]{:S(2)}) collective-permute-start(bf16[512,353]{0,1:T(8,128)(2,1)S(1)} %get-tuple-element.16), channel_id=1, source_target_pairs={{8,0},{16,8},{24,16},{32,24},{40,32},{48,40},{56,48},{64,56},{72,6... | collective-permute-start | bytes 1084424 | tf_op jit(solution)/shard_map/ppermute | solution.py:14
  27.5 26.7 %collective-permute-start.2 = (bf16[512,353]{0,1:T(8,128)(2,1)S(1)}, bf16[512,353]{0,1:T(8,128)(2,1)}, u32[]{:S(2)}, u32[]{:S(2)}) collective-permute-start(bf16[512,353]{0,1:T(8,128)(2,1)S(1)} %get-tuple-element.16), channel_id=1, source_target_pairs={{0,16},{8,24},{16,32},{24,40},{32,48},{40,56},{48,64},{56,72},{64,... | collective-permute-start | bytes 1084424 | tf_op jit(solution)/shard_map/ppermute | solution.py:14
  29.5 32.9 %collective-permute-start.3 = (bf16[512,353]{0,1:T(8,128)(2,1)S(1)}, bf16[512,353]{0,1:T(8,128)(2,1)S(1)}, u32[]{:S(2)}, u32[]{:S(2)}) collective-permute-start(bf16[512,353]{0,1:T(8,128)(2,1)S(1)} %get-tuple-element.16), channel_id=1, source_target_pairs={{16,0},{24,8},{32,16},{40,24},{48,32},{56,40},{64,48},{72,56},{80,... | collective-permute-start | bytes 1084424 | tf_op jit(solution)/shard_map/ppermute | solution.py:14
  35.5 27.7 %collective-permute-start.4 = (bf16[512,353]{0,1:T(8,128)(2,1)S(1)}, bf16[512,353]{0,1:T(8,128)(2,1)S(1)}, u32[]{:S(2)}, u32[]{:S(2)}) collective-permute-start(bf16[512,353]{0,1:T(8,128)(2,1)S(1)} %get-tuple-element.16), channel_id=1, source_target_pairs={{0,24},{8,32},{16,40},{24,48},{32,56},{40,64},{48,72},{56,80},{64,... | collective-permute-start | bytes 1084424 | tf_op jit(solution)/shard_map/ppermute | solution.py:14
  40.0 56.2 %collective-permute-start.5 = (bf16[512,353]{0,1:T(8,128)(2,1)S(1)}, bf16[512,353]{0,1:T(8,128)(2,1)S(1)}, u32[]{:S(2)}, u32[]{:S(2)}) collective-permute-start(bf16[512,353]{0,1:T(8,128)(2,1)S(1)} %get-tuple-element.16), channel_id=1, source_target_pairs={{24,0},{32,8},{40,16},{48,24},{56,32},{64,40},{72,48},{80,56},{88,... | collective-permute-start | bytes 1084424 | tf_op jit(solution)/shard_map/ppermute | solution.py:14
  50.6 46.4 %collective-permute-start.6 = (bf16[512,353]{0,1:T(8,128)(2,1)S(1)}, bf16[512,353]{0,1:T(8,128)(2,1)S(1)}, u32[]{:S(2)}, u32[]{:S(2)}) collective-permute-start(bf16[512,353]{0,1:T(8,128)(2,1)S(1)} %get-tuple-element.16), channel_id=1, source_target_pairs={{0,32},{8,40},{16,48},{24,56},{32,64},{40,72},{48,80},{56,88},{64,... | collective-permute-start | bytes 1084424 | tf_op jit(solution)/shard_map/ppermute | solution.py:14
  54.3 43.5 %collective-permute-start.7 = (bf16[512,353]{0,1:T(8,128)(2,1)S(1)}, bf16[512,353]{0,1:T(8,128)(2,1)S(1)}, u32[]{:S(2)}, u32[]{:S(2)}) collective-permute-start(bf16[512,353]{0,1:T(8,128)(2,1)S(1)} %get-tuple-element.16), channel_id=1, source_target_pairs={{32,0},{40,8},{48,16},{56,24},{64,32},{72,40},{80,48},{88,56},{96,... | collective-permute-start | bytes 1084424 | tf_op jit(solution)/shard_map/ppermute | solution.py:14
  129.5 3.0 copy-start.2
  134.2 72.3 %all-to-all-start = ((bf16[8,64,1408]{2,1,0:T(8,128)(2,1)}), bf16[8,64,1408]{2,1,0:T(8,128)(2,1)}, u32[]{:S(2)}, u32[]{:S(2)}) async-start(bf16[8,64,1408]{2,1,0:T(8,128)(2,1)} %bitcast.46), calls=%async_computation | async-start | bytes 2883584 | tf_op jit(solution)/shard_map/all_to_all | solution.py:110
  147.3 62.3 %copy-start.3 = (f32[1408]{0:T(1024)S(1)}, f32[1408]{0:T(1024)}, u32[]{:S(2)}) copy-start(f32[1408]{0:T(1024)} %param.18) | copy-start | bytes 16900
  147.3 62.3 %copy-start.4 = (f32[1408]{0:T(1024)S(1)}, f32[1408]{0:T(1024)}, u32[]{:S(2)}) copy-start(f32[1408]{0:T(1024)} %param.17) | copy-start | bytes 16900
  342.4 1.2 collective-permute-start.8
  343.8 3.6 collective-permute-start.9
  347.5 4.5 %collective-permute-start.10 = (f32[48]{0:T(128)S(1)}, f32[48]{0:T(128)S(1)}, u32[]{:S(2)}, u32[]{:S(2)}) collective-permute-start(f32[48]{0:T(128)S(1)} %pad_maximum_fusion.3), channel_id=1, source_target_pairs={{0,4},{1,5},{2,6},{3,7},{4,0},{5,1},{6,2},{7,3},{8,12},{9,13},{10,... | collective-permute-start | bytes 584 | tf_op jit(solution)/shard_map/ppermute | solution.py:30
  352.2 7.5 %collective-permute-start.11 = (f32[48]{0:T(128)S(1)}, f32[48]{0:T(128)S(1)}, u32[]{:S(2)}, u32[]{:S(2)}) collective-permute-start(f32[48]{0:T(128)S(1)} %pad_maximum_fusion.4), channel_id=1, source_target_pairs={{0,8},{8,0},{16,24},{24,16},{32,40},{40,32},{48,56},{56,48},{64,72... | collective-permute-start | bytes 584 | tf_op jit(solution)/shard_map/ppermute | solution.py:30
  359.8 3.6 collective-permute-start.12
  363.6 5.1 %collective-permute-start.13 = (f32[48]{0:T(128)S(1)}, f32[48]{0:T(128)S(1)}, u32[]{:S(2)}, u32[]{:S(2)}) collective-permute-start(f32[48]{0:T(128)S(1)} %pad_maximum_fusion.6), channel_id=1, source_target_pairs={{0,32},{8,40},{16,48},{24,56},{32,0},{40,8},{48,16},{56,24},{64,96... | collective-permute-start | bytes 584 | tf_op jit(solution)/shard_map/ppermute | solution.py:30
  368.8 3.6 collective-permute-start.14
  372.5 5.1 %collective-permute-start.15 = (f32[48]{0:T(128)S(1)}, f32[48]{0:T(128)S(1)}, u32[]{:S(2)}, u32[]{:S(2)}) collective-permute-start(f32[48]{0:T(128)S(1)} %pad_maximum_fusion.8), channel_id=1, source_target_pairs={{0,128},{8,136},{16,144},{24,152},{32,160},{40,168},{48,176},{56,1... | collective-permute-start | bytes 584 | tf_op jit(solution)/shard_map/ppermute | solution.py:30
  378.2 0.9 copy-start.6
Sparse Core Ops, SparseCore 0:
  11.4 172.8 all-gather.1

commit v4 on v3

--- a/solution.py
+++ b/solution.py
@@ -110,12 +110,12 @@
     attn_pieces = lax.all_to_all(attn_part.reshape(n_head, share, width), "head", 0, 0, tiled=True)
     x_mine = lax.dynamic_slice_in_dim(x_in, lax.axis_index("head") * share, share, 0)
     h_one = x_mine + jnp.sum(attn_pieces.astype(jnp.float32), axis=0)
-    h_one, full_proj_weight = lax.optimization_barrier((h_one, full_proj_weight))
     n_two = gather_rows(layer_norm(h_one, ln2_gain, ln2_bias).astype(jnp.bfloat16), n_head)
     hidden = jax.nn.gelu(
         jnp.dot(n_two, fc1_weight, preferred_element_type=jnp.float32), approximate=False
     ).astype(jnp.bfloat16)
     mlp_part = jnp.dot(hidden, fc2_weight, preferred_element_type=jnp.float32).astype(jnp.bfloat16)
+    mlp_part, full_proj_weight = lax.optimization_barrier((mlp_part, full_proj_weight))
     pieces = lax.all_to_all(mlp_part.reshape(n_head, share, width), "head", 0, 0, tiled=True)
     layer_mine = (h_one + jnp.sum(pieces.astype(jnp.float32), axis=0)).astype(jnp.bfloat16)
     layer = gather_rows(layer_mine, n_head)

time: 387 us -> 398 us (1.028)
  waiting for transfers between devices: 113 us -> 121 us
    all_to_all x1, waiting for transfers between devices: 59.2 us -> 73.1 us  [per_device(): lax.all_to_all(attn_part.reshape(n_head, share, width), 'head', 0, 0, til...]
    ppermute x8, waiting for transfers between devices: 32.2 us -> 26.3 us  [passed_along(): return lax.ppermute(x, axis, pairs)]
where the time goes in v4:
time: 398 us; the launch traced here: 397 us
  waiting for transfers between devices  121 us (30%)
  blocking collectives  115 us (29%)
  starting transfers between devices  68.2 us (17%)
  other arithmetic  34.1 us (9%)
  matrix products  29 us (7%)
  local copies, waits for them, and re-layouts  15.9 us (4%)
  between operations  14.4 us (4%)
    all_to_all x2, blocking collectives, gather_rows(): got = lax.all_to_all(spread, 'head', 0, 0, tiled=True)  76.3 us
    all_to_all x1, waiting for transfers between devices, per_device(): lax.all_to_all(attn_part.reshape(n_head, share, width), 'head', 0, 0, til...  73.1 us
    ppermute x8, starting transfers between devices, passed_along(): return lax.ppermute(x, axis, pairs)  42.7 us
    all_to_all x1, blocking collectives, per_device(): lax.all_to_all(mlp_part.reshape(n_head, share, width), 'head', 0, 0, tile...  38.5 us
    ppermute x8, waiting for transfers between devices, passed_along(): return lax.ppermute(x, axis, pairs)  26.3 us
    ppermute x8, waiting for transfers between devices, butterfly(): other = lax.ppermute(both, axis, pairs)  21.3 us
    sub x1, other arithmetic, per_device(): weights = jnp.where(mask, jnp.exp(scores - top[..., None]), 0.0)  18.4 us
    ppermute x8, starting transfers between devices, butterfly(): other = lax.ppermute(both, axis, pairs)  12.8 us
  transfers between devices with their start and end apart: 18, of which 10 were waited for; matrix products, arithmetic and copies ran while one was open for 15% of the time, Pallas kernels for 0%

profile of v4, /device:TPU:2, one launch (start us, length us, event | category | flops | bytes accessed | tf_op | source)
XLA Modules:
  0.0 397.1 jit_solution(4708125683894980021)
XLA Ops:
  10.6 2.6 fusion.20
  14.2 9.1 %collective-permute-start = (bf16[512,353]{0,1:T(8,128)(2,1)S(1)}, bf16[512,353]{0,1:T(8,128)(2,1)}, u32[]{:S(2)}, u32[]{:S(2)}) collective-permute-start(bf16[512,353]{0,1:T(8,128)(2,1)S(1)} %get-tuple-element.18), channel_id=1, source_target_pairs={{0,8},{8,16},{16,24},{24,32},{32,40},{40,48},{48,56},{56,64},{64,7... | collective-permute-start | bytes 1084424 | tf_op jit(solution)/shard_map/ppermute | solution.py:14
  23.3 4.3 %collective-permute-start.1 = (bf16[512,353]{0,1:T(8,128)(2,1)S(1)}, bf16[512,353]{0,1:T(8,128)(2,1)}, u32[]{:S(2)}, u32[]{:S(2)}) collective-permute-start(bf16[512,353]{0,1:T(8,128)(2,1)S(1)} %get-tuple-element.18), channel_id=1, source_target_pairs={{8,0},{16,8},{24,16},{32,24},{40,32},{48,40},{56,48},{64,56},{72,6... | collective-permute-start | bytes 1084424 | tf_op jit(solution)/shard_map/ppermute | solution.py:14
  27.6 1.9 collective-permute-start.2
  29.5 6.0 %collective-permute-start.3 = (bf16[512,353]{0,1:T(8,128)(2,1)S(1)}, bf16[512,353]{0,1:T(8,128)(2,1)S(1)}, u32[]{:S(2)}, u32[]{:S(2)}) collective-permute-start(bf16[512,353]{0,1:T(8,128)(2,1)S(1)} %get-tuple-element.18), channel_id=1, source_target_pairs={{16,0},{24,8},{32,16},{40,24},{48,32},{56,40},{64,48},{72,56},{80,... | collective-permute-start | bytes 1084424 | tf_op jit(solution)/shard_map/ppermute | solution.py:14
  35.6 4.3 %collective-permute-start.4 = (bf16[512,353]{0,1:T(8,128)(2,1)S(1)}, bf16[512,353]{0,1:T(8,128)(2,1)S(1)}, u32[]{:S(2)}, u32[]{:S(2)}) collective-permute-start(bf16[512,353]{0,1:T(8,128)(2,1)S(1)} %get-tuple-element.18), channel_id=1, source_target_pairs={{0,24},{8,32},{16,40},{24,48},{32,56},{40,64},{48,72},{56,80},{64,... | collective-permute-start | bytes 1084424 | tf_op jit(solution)/shard_map/ppermute | solution.py:14
  40.1 8.7 %collective-permute-start.5 = (bf16[512,353]{0,1:T(8,128)(2,1)S(1)}, bf16[512,353]{0,1:T(8,128)(2,1)S(1)}, u32[]{:S(2)}, u32[]{:S(2)}) collective-permute-start(bf16[512,353]{0,1:T(8,128)(2,1)S(1)} %get-tuple-element.18), channel_id=1, source_target_pairs={{24,0},{32,8},{40,16},{48,24},{56,32},{64,40},{72,48},{80,56},{88,... | collective-permute-start | bytes 1084424 | tf_op jit(solution)/shard_map/ppermute | solution.py:14
  54.4 6.3 %collective-permute-start.7 = (bf16[512,353]{0,1:T(8,128)(2,1)S(1)}, bf16[512,353]{0,1:T(8,128)(2,1)S(1)}, u32[]{:S(2)}, u32[]{:S(2)}) collective-permute-start(bf16[512,353]{0,1:T(8,128)(2,1)S(1)} %get-tuple-element.18), channel_id=1, source_target_pairs={{32,0},{40,8},{48,16},{56,24},{64,32},{72,40},{80,48},{88,56},{96,... | collective-permute-start | bytes 1084424 | tf_op jit(solution)/shard_map/ppermute | solution.py:14
  64.2 26.3 %collective-permute-done.5 = bf16[512,353]{0,1:T(8,128)(2,1)S(1)} collective-permute-done((bf16[512,353]{0,1:T(8,128)(2,1)S(1)}, bf16[512,353]{0,1:T(8,128)(2,1)S(1)}, u32[]{:S(2)}, u32[]{:S(2)}) %collective-permute-start.5) | collective-permute-done | bytes 361504 | tf_op jit(solution)/shard_map/ppermute | solution.py:14
  92.9 2.1 fusion.104
  97.4 7.9 %fusion.109 = f32[2,512,4608]{2,1,0:T(8,128)} fusion(bf16[512,2,88]{0,2,1:T(8,128)(2,1)S(1)} %bitcast.50, bf16[4608,2,88]{0,2,1:T(8,128)(2,1)S(1)} %bitcast.44), kind=kOutput, calls=%fused_computation.176 | convolution fusion | flops 830472192 | bytes 20676608 | tf_op jit(solution)/shard_map/rhe,phe->hrp/dot_general | solution.py:91
  105.3 18.4 %fusion.106 = (f32[2,512]{1,0:T(2,128)S(1)}, bf16[2,512,4608]{2,1,0:T(8,128)(2,1)S(1)}) fusion(f32[2,512,4608]{2,1,0:T(8,128)} %fusion.109, pred[512,4608]{1,0:T(8,128)(4,1)S(1)} %broadcast_compare_fusion), kind=kOutput, calls=%fused_computation.174 | output fusion | flops 33034752 | bytes 30674944 | tf_op jit(solution)/shard_map/sub | solution.py:95
  123.7 3.0 fusion.31
  128.4 12.7 %all-to-all-start = ((bf16[8,64,1408]{2,1,0:T(8,128)(2,1)}), bf16[8,64,1408]{2,1,0:T(8,128)(2,1)}, u32[]{:S(2)}, u32[]{:S(2)}) async-start(bf16[8,64,1408]{2,1,0:T(8,128)(2,1)} %bitcast.46), calls=%async_computation | async-start | bytes 2883584 | tf_op jit(solution)/shard_map/all_to_all | solution.py:110
  141.1 3.4 convert_element_type.70
  144.5 73.1 %all-to-all-done = bf16[8,64,1408]{2,1,0:T(8,128)(2,1)} async-done(((bf16[8,64,1408]{2,1,0:T(8,128)(2,1)}), bf16[8,64,1408]{2,1,0:T(8,128)(2,1)}, u32[]{:S(2)}, u32[]{:S(2)}) %all-to-all-start) | async-done | bytes 1441824 | tf_op jit(solution)/shard_map/all_to_all | solution.py:110
  220.9 38.1 %all_to_all.20 = bf16[8,64,1408]{2,1,0:T(8,128)(2,1)} all-to-all(bf16[8,64,1408]{2,1,0:T(8,128)(2,1)S(1)} %broadcast_in_dim.41), channel_id=1, replica_groups=mesh['blk'=32,'head'=8] {'head'}, dimensions={0} | all-to-all | bytes 2883584 | tf_op jit(solution)/shard_map/all_to_all | solution.py:40
  259.0 9.4 %convolution_convert_fusion = bf16[512,1408]{1,0:T(8,128)(2,1)} fusion(bf16[768,1408]{1,0:T(8,128)(2,1)S(1)} %copy-done, bf16[512,1408]{1,0:T(8,128)(2,1)} %bitcast.48, bf16[1408,768]{1,0:T(8,128)(2,1)} %param.19), kind=kOutput, calls=%fused_computation.11 | convolution fusion | flops 2240872448 | bytes 7208960 | tf_op jit(solution)/shard_map/dot_general | solution.py:117
  268.5 38.5 %all_to_all.21 = bf16[8,64,1408]{2,1,0:T(8,128)(2,1)S(1)} all-to-all(bf16[8,64,1408]{2,1,0:T(8,128)(2,1)} %bitcast.47), channel_id=1, replica_groups=mesh['blk'=32,'head'=8] {'head'}, dimensions={0} | all-to-all | bytes 2883584 | tf_op jit(solution)/shard_map/all_to_all | solution.py:119
  307.3 38.1 %all_to_all.22 = bf16[8,64,1408]{2,1,0:T(8,128)(2,1)} all-to-all(bf16[8,64,1408]{2,1,0:T(8,128)(2,1)S(1)} %broadcast_in_dim.68), channel_id=1, replica_groups=mesh['blk'=32,'head'=8] {'head'}, dimensions={0} | all-to-all | bytes 2883584 | tf_op jit(solution)/shard_map/all_to_all | solution.py:40
  345.4 3.6 reshape_reshape.3
  349.0 4.1 %abs_reduce_fusion = (f32[128]{0:T(128)S(1)}, f32[128]{0:T(128)S(1)}, f32[128,512]{1,0:T(8,128)S(1)}) fusion(bf16[128,5632]{1,0:T(8,128)(2,1)} %reshape_reshape.3, bf16[5632,512]{1,0:T(8,128)(2,1)} %all-gather.2.cloned.1.call-done), kind=kOutput, calls=%fused_computation.84 | convolution fusion | flops 738459392 | bytes 7472128 | tf_op jit(solution)/shard_map/dot_general | solution.py:123
  355.1 3.4 collective-permute-done.9
  358.6 4.5 %collective-permute-done.10 = f32[48]{0:T(128)S(1)} collective-permute-done((f32[48]{0:T(128)S(1)}, f32[48]{0:T(128)S(1)}, u32[]{:S(2)}, u32[]{:S(2)}) %collective-permute-start.10) | collective-permute-done | bytes 224 | tf_op jit(solution)/shard_map/ppermute | solution.py:30
  363.3 4.6 %collective-permute-start.11 = (f32[48]{0:T(128)S(1)}, f32[48]{0:T(128)S(1)}, u32[]{:S(2)}, u32[]{:S(2)}) collective-permute-start(f32[48]{0:T(128)S(1)} %pad_maximum_fusion.4), channel_id=1, source_target_pairs={{0,8},{8,0},{16,24},{24,16},{32,40},{40,32},{48,56},{56,48},{64,72... | collective-permute-start | bytes 584 | tf_op jit(solution)/shard_map/ppermute | solution.py:30
  367.8 2.9 collective-permute-done.11
  370.9 2.1 collective-permute-start.12
  374.7 2.7 collective-permute-start.13
  377.4 2.4 collective-permute-done.13
  380.5 3.0 collective-permute-done.14
  383.7 2.6 collective-permute-start.15
  386.2 2.5 collective-permute-done.15
  (96 shorter events, 30.0 us)
Async XLA Ops:
  7.2 251.8 %copy-start = (bf16[768,1408]{1,0:T(8,128)(2,1)S(1)}, bf16[768,1408]{1,0:T(8,128)(2,1)}, u32[]{:S(2)}) copy-start(bf16[768,1408]{1,0:T(8,128)(2,1)} %param.20) | copy-start | bytes 6488068
  7.2 3.4 copy-start.7
  7.2 3.4 copy-start.8
  7.2 261.3 %all-gather.2.cloned.1.call-start = ((), (), s32[]{:S(2)}) async-start(), calls=%async_computation.4 | async-start | bytes 5947392 | tf_op jit(solution)/shard_map/all_gather | solution.py:108
  8.3 1.8 copy-start.1
  14.2 26.0 %collective-permute-start = (bf16[512,353]{0,1:T(8,128)(2,1)S(1)}, bf16[512,353]{0,1:T(8,128)(2,1)}, u32[]{:S(2)}, u32[]{:S(2)}) collective-permute-start(bf16[512,353]{0,1:T(8,128)(2,1)S(1)} %get-tuple-element.18), channel_id=1, source_target_pairs={{0,8},{8,16},{16,24},{24,32},{32,40},{40,48},{48,56},{56,64},{64,7... | collective-permute-start | bytes 1084424 | tf_op jit(solution)/shard_map/ppermute | solution.py:14
  23.3 27.4 %collective-permute-start.1 = (bf16[512,353]{0,1:T(8,128)(2,1)S(1)}, bf16[512,353]{0,1:T(8,128)(2,1)}, u32[]{:S(2)}, u32[]{:S(2)}) collective-permute-start(bf16[512,353]{0,1:T(8,128)(2,1)S(1)} %get-tuple-element.18), channel_id=1, source_target_pairs={{8,0},{16,8},{24,16},{32,24},{40,32},{48,40},{56,48},{64,56},{72,6... | collective-permute-start | bytes 1084424 | tf_op jit(solution)/shard_map/ppermute | solution.py:14
  27.6 26.8 %collective-permute-start.2 = (bf16[512,353]{0,1:T(8,128)(2,1)S(1)}, bf16[512,353]{0,1:T(8,128)(2,1)}, u32[]{:S(2)}, u32[]{:S(2)}) collective-permute-start(bf16[512,353]{0,1:T(8,128)(2,1)S(1)} %get-tuple-element.18), channel_id=1, source_target_pairs={{0,16},{8,24},{16,32},{24,40},{32,48},{40,56},{48,64},{56,72},{64,... | collective-permute-start | bytes 1084424 | tf_op jit(solution)/shard_map/ppermute | solution.py:14
  29.5 33.0 %collective-permute-start.3 = (bf16[512,353]{0,1:T(8,128)(2,1)S(1)}, bf16[512,353]{0,1:T(8,128)(2,1)S(1)}, u32[]{:S(2)}, u32[]{:S(2)}) collective-permute-start(bf16[512,353]{0,1:T(8,128)(2,1)S(1)} %get-tuple-element.18), channel_id=1, source_target_pairs={{16,0},{24,8},{32,16},{40,24},{48,32},{56,40},{64,48},{72,56},{80,... | collective-permute-start | bytes 1084424 | tf_op jit(solution)/shard_map/ppermute | solution.py:14
  35.6 27.8 %collective-permute-start.4 = (bf16[512,353]{0,1:T(8,128)(2,1)S(1)}, bf16[512,353]{0,1:T(8,128)(2,1)S(1)}, u32[]{:S(2)}, u32[]{:S(2)}) collective-permute-start(bf16[512,353]{0,1:T(8,128)(2,1)S(1)} %get-tuple-element.18), channel_id=1, source_target_pairs={{0,24},{8,32},{16,40},{24,48},{32,56},{40,64},{48,72},{56,80},{64,... | collective-permute-start | bytes 1084424 | tf_op jit(solution)/shard_map/ppermute | solution.py:14
  40.1 50.4 %collective-permute-start.5 = (bf16[512,353]{0,1:T(8,128)(2,1)S(1)}, bf16[512,353]{0,1:T(8,128)(2,1)S(1)}, u32[]{:S(2)}, u32[]{:S(2)}) collective-permute-start(bf16[512,353]{0,1:T(8,128)(2,1)S(1)} %get-tuple-element.18), channel_id=1, source_target_pairs={{24,0},{32,8},{40,16},{48,24},{56,32},{64,40},{72,48},{80,56},{88,... | collective-permute-start | bytes 1084424 | tf_op jit(solution)/shard_map/ppermute | solution.py:14
  50.7 40.6 %collective-permute-start.6 = (bf16[512,353]{0,1:T(8,128)(2,1)S(1)}, bf16[512,353]{0,1:T(8,128)(2,1)S(1)}, u32[]{:S(2)}, u32[]{:S(2)}) collective-permute-start(bf16[512,353]{0,1:T(8,128)(2,1)S(1)} %get-tuple-element.18), channel_id=1, source_target_pairs={{0,32},{8,40},{16,48},{24,56},{32,64},{40,72},{48,80},{56,88},{64,... | collective-permute-start | bytes 1084424 | tf_op jit(solution)/shard_map/ppermute | solution.py:14
  54.4 37.7 %collective-permute-start.7 = (bf16[512,353]{0,1:T(8,128)(2,1)S(1)}, bf16[512,353]{0,1:T(8,128)(2,1)S(1)}, u32[]{:S(2)}, u32[]{:S(2)}) collective-permute-start(bf16[512,353]{0,1:T(8,128)(2,1)S(1)} %get-tuple-element.18), channel_id=1, source_target_pairs={{32,0},{40,8},{48,16},{56,24},{64,32},{72,40},{80,48},{88,56},{96,... | collective-permute-start | bytes 1084424 | tf_op jit(solution)/shard_map/ppermute | solution.py:14
  123.7 3.0 copy-start.2
  128.4 89.3 %all-to-all-start = ((bf16[8,64,1408]{2,1,0:T(8,128)(2,1)}), bf16[8,64,1408]{2,1,0:T(8,128)(2,1)}, u32[]{:S(2)}, u32[]{:S(2)}) async-start(bf16[8,64,1408]{2,1,0:T(8,128)(2,1)} %bitcast.46), calls=%async_computation | async-start | bytes 2883584 | tf_op jit(solution)/shard_map/all_to_all | solution.py:110
  144.5 76.1 %copy-start.3 = (f32[1408]{0:T(1024)S(1)}, f32[1408]{0:T(1024)}, u32[]{:S(2)}) copy-start(f32[1408]{0:T(1024)} %param.18) | copy-start | bytes 16900
  144.5 76.1 %copy-start.4 = (f32[1408]{0:T(1024)S(1)}, f32[1408]{0:T(1024)}, u32[]{:S(2)}) copy-start(f32[1408]{0:T(1024)} %param.17) | copy-start | bytes 16900
  349.0 4.1 %copy-start.5 = (s32[128]{0:T(128)S(1)}, s32[128]{0:T(128)}, u32[]{:S(2)}) copy-start(s32[128]{0:T(128)} %param.12) | copy-start | bytes 1540
  353.5 1.2 collective-permute-start.8
  354.9 3.6 collective-permute-start.9
  358.6 4.5 %collective-permute-start.10 = (f32[48]{0:T(128)S(1)}, f32[48]{0:T(128)S(1)}, u32[]{:S(2)}, u32[]{:S(2)}) collective-permute-start(f32[48]{0:T(128)S(1)} %pad_maximum_fusion.3), channel_id=1, source_target_pairs={{0,4},{1,5},{2,6},{3,7},{4,0},{5,1},{6,2},{7,3},{8,12},{9,13},{10,... | collective-permute-start | bytes 584 | tf_op jit(solution)/shard_map/ppermute | solution.py:30
  363.3 7.5 %collective-permute-start.11 = (f32[48]{0:T(128)S(1)}, f32[48]{0:T(128)S(1)}, u32[]{:S(2)}, u32[]{:S(2)}) collective-permute-start(f32[48]{0:T(128)S(1)} %pad_maximum_fusion.4), channel_id=1, source_target_pairs={{0,8},{8,0},{16,24},{24,16},{32,40},{40,32},{48,56},{56,48},{64,72... | collective-permute-start | bytes 584 | tf_op jit(solution)/shard_map/ppermute | solution.py:30
  370.9 3.6 collective-permute-start.12
  374.7 5.1 %collective-permute-start.13 = (f32[48]{0:T(128)S(1)}, f32[48]{0:T(128)S(1)}, u32[]{:S(2)}, u32[]{:S(2)}) collective-permute-start(f32[48]{0:T(128)S(1)} %pad_maximum_fusion.6), channel_id=1, source_target_pairs={{0,32},{8,40},{16,48},{24,56},{32,0},{40,8},{48,16},{56,24},{64,96... | collective-permute-start | bytes 584 | tf_op jit(solution)/shard_map/ppermute | solution.py:30
  379.9 3.6 collective-permute-start.14
  383.7 5.1 %collective-permute-start.15 = (f32[48]{0:T(128)S(1)}, f32[48]{0:T(128)S(1)}, u32[]{:S(2)}, u32[]{:S(2)}) collective-permute-start(f32[48]{0:T(128)S(1)} %pad_maximum_fusion.8), channel_id=1, source_target_pairs={{0,128},{8,136},{16,144},{24,152},{32,160},{40,168},{48,176},{56,1... | collective-permute-start | bytes 584 | tf_op jit(solution)/shard_map/ppermute | solution.py:30
  389.3 0.9 copy-start.6
Sparse Core Ops, SparseCore 0:
  40.0 176.7 all-gather.1

commit v5 on v3

--- a/solution.py
+++ b/solution.py
@@ -118,8 +118,7 @@
     mlp_part = jnp.dot(hidden, fc2_weight, preferred_element_type=jnp.float32).astype(jnp.bfloat16)
     pieces = lax.all_to_all(mlp_part.reshape(n_head, share, width), "head", 0, 0, tiled=True)
     layer_mine = (h_one + jnp.sum(pieces.astype(jnp.float32), axis=0)).astype(jnp.bfloat16)
-    layer = gather_rows(layer_mine, n_head)
-    grouped = layer.reshape(rows // 4, 4 * layer.shape[1])
+    grouped = gather_rows(layer_mine.reshape(share // 4, 4 * width), n_head)
     proj = jnp.dot(
         grouped,
         full_proj_weight,

time: 387 us -> 382 us (0.987)
  no operation moved by 1% of the time
where the time goes in v5:
time: 382 us; the launch traced here: 381 us
  blocking collectives  114 us (30%)
  waiting for transfers between devices  113 us (30%)
  starting transfers between devices  65.4 us (17%)
  other arithmetic  33.1 us (9%)
  matrix products  28.7 us (8%)
  between operations  14.4 us (4%)
  local copies, waits for them, and re-layouts  12.4 us (3%)
    all_to_all x2, blocking collectives, gather_rows(): got = lax.all_to_all(spread, 'head', 0, 0, tiled=True)  75.5 us
    all_to_all x1, waiting for transfers between devices, per_device(): lax.all_to_all(attn_part.reshape(n_head, share, width), 'head', 0, 0, til...  59.2 us
    ppermute x8, starting transfers between devices, passed_along(): return lax.ppermute(x, axis, pairs)  42.7 us
    all_to_all x1, blocking collectives, per_device(): lax.all_to_all(mlp_part.reshape(n_head, share, width), 'head', 0, 0, tile...  38.5 us
    ppermute x8, waiting for transfers between devices, passed_along(): return lax.ppermute(x, axis, pairs)  32.2 us
    ppermute x8, waiting for transfers between devices, butterfly(): other = lax.ppermute(both, axis, pairs)  21.3 us
    sub x1, other arithmetic, per_device(): weights = jnp.where(mask, jnp.exp(scores - top[..., None]), 0.0)  18.4 us
    ppermute x8, starting transfers between devices, butterfly(): other = lax.ppermute(both, axis, pairs)  12.9 us
  transfers between devices with their start and end apart: 18, of which 10 were waited for; matrix products, arithmetic and copies ran while one was open for 15% of the time, Pallas kernels for 0%

profile of v5, /device:TPU:2, one launch (start us, length us, event | category | flops | bytes accessed | tf_op | source)
XLA Modules:
  0.0 381.3 jit_solution(5592622119931128887)
XLA Ops:
  10.3 2.6 fusion.20
  14.1 9.1 %collective-permute-start = (bf16[512,353]{0,1:T(8,128)(2,1)S(1)}, bf16[512,353]{0,1:T(8,128)(2,1)}, u32[]{:S(2)}, u32[]{:S(2)}) collective-permute-start(bf16[512,353]{0,1:T(8,128)(2,1)S(1)} %get-tuple-element.16), channel_id=1, source_target_pairs={{0,8},{8,16},{16,24},{24,32},{32,40},{40,48},{48,56},{56,64},{64,7... | collective-permute-start | bytes 1084424 | tf_op jit(solution)/shard_map/ppermute | solution.py:14
  23.2 4.3 %collective-permute-start.1 = (bf16[512,353]{0,1:T(8,128)(2,1)S(1)}, bf16[512,353]{0,1:T(8,128)(2,1)}, u32[]{:S(2)}, u32[]{:S(2)}) collective-permute-start(bf16[512,353]{0,1:T(8,128)(2,1)S(1)} %get-tuple-element.16), channel_id=1, source_target_pairs={{8,0},{16,8},{24,16},{32,24},{40,32},{48,40},{56,48},{64,56},{72,6... | collective-permute-start | bytes 1084424 | tf_op jit(solution)/shard_map/ppermute | solution.py:14
  27.5 1.9 collective-permute-start.2
  29.5 6.0 %collective-permute-start.3 = (bf16[512,353]{0,1:T(8,128)(2,1)S(1)}, bf16[512,353]{0,1:T(8,128)(2,1)S(1)}, u32[]{:S(2)}, u32[]{:S(2)}) collective-permute-start(bf16[512,353]{0,1:T(8,128)(2,1)S(1)} %get-tuple-element.16), channel_id=1, source_target_pairs={{16,0},{24,8},{32,16},{40,24},{48,32},{56,40},{64,48},{72,56},{80,... | collective-permute-start | bytes 1084424 | tf_op jit(solution)/shard_map/ppermute | solution.py:14
  35.5 4.3 %collective-permute-start.4 = (bf16[512,353]{0,1:T(8,128)(2,1)S(1)}, bf16[512,353]{0,1:T(8,128)(2,1)S(1)}, u32[]{:S(2)}, u32[]{:S(2)}) collective-permute-start(bf16[512,353]{0,1:T(8,128)(2,1)S(1)} %get-tuple-element.16), channel_id=1, source_target_pairs={{0,24},{8,32},{16,40},{24,48},{32,56},{40,64},{48,72},{56,80},{64,... | collective-permute-start | bytes 1084424 | tf_op jit(solution)/shard_map/ppermute | solution.py:14
  40.0 8.7 %collective-permute-start.5 = (bf16[512,353]{0,1:T(8,128)(2,1)S(1)}, bf16[512,353]{0,1:T(8,128)(2,1)S(1)}, u32[]{:S(2)}, u32[]{:S(2)}) collective-permute-start(bf16[512,353]{0,1:T(8,128)(2,1)S(1)} %get-tuple-element.16), channel_id=1, source_target_pairs={{24,0},{32,8},{40,16},{48,24},{56,32},{64,40},{72,48},{80,56},{88,... | collective-permute-start | bytes 1084424 | tf_op jit(solution)/shard_map/ppermute | solution.py:14
  50.6 1.9 collective-permute-start.6
  54.3 6.3 %collective-permute-start.7 = (bf16[512,353]{0,1:T(8,128)(2,1)S(1)}, bf16[512,353]{0,1:T(8,128)(2,1)S(1)}, u32[]{:S(2)}, u32[]{:S(2)}) collective-permute-start(bf16[512,353]{0,1:T(8,128)(2,1)S(1)} %get-tuple-element.16), channel_id=1, source_target_pairs={{32,0},{40,8},{48,16},{56,24},{64,32},{72,40},{80,48},{88,56},{96,... | collective-permute-start | bytes 1084424 | tf_op jit(solution)/shard_map/ppermute | solution.py:14
  64.1 32.1 %collective-permute-done.5 = bf16[512,353]{0,1:T(8,128)(2,1)S(1)} collective-permute-done((bf16[512,353]{0,1:T(8,128)(2,1)S(1)}, bf16[512,353]{0,1:T(8,128)(2,1)S(1)}, u32[]{:S(2)}, u32[]{:S(2)}) %collective-permute-start.5) | collective-permute-done | bytes 361504 | tf_op jit(solution)/shard_map/ppermute | solution.py:14
  99.6 2.1 fusion.103
  101.7 8.1 %fusion.108 = f32[2,512,4608]{2,1,0:T(8,128)} fusion(bf16[512,2,88]{0,2,1:T(8,128)(2,1)S(1)} %bitcast.52, bf16[4608,2,88]{0,2,1:T(8,128)(2,1)S(1)} %bitcast.45), kind=kOutput, calls=%fused_computation.175 | convolution fusion | flops 830472192 | bytes 20676608 | tf_op jit(solution)/shard_map/rhe,phe->hrp/dot_general | solution.py:91
  111.1 18.4 %fusion.105 = (f32[2,512]{1,0:T(2,128)S(1)}, bf16[2,512,4608]{2,1,0:T(8,128)(2,1)S(1)}) fusion(f32[2,512,4608]{2,1,0:T(8,128)} %fusion.108, pred[512,4608]{1,0:T(8,128)(4,1)S(1)} %broadcast_compare_fusion), kind=kOutput, calls=%fused_computation.173 | output fusion | flops 33034752 | bytes 30674944 | tf_op jit(solution)/shard_map/sub | solution.py:95
  129.5 3.0 fusion.31
  134.2 9.9 %all-to-all-start = ((bf16[8,64,1408]{2,1,0:T(8,128)(2,1)}), bf16[8,64,1408]{2,1,0:T(8,128)(2,1)}, u32[]{:S(2)}, u32[]{:S(2)}) async-start(bf16[8,64,1408]{2,1,0:T(8,128)(2,1)} %bitcast.47), calls=%async_computation | async-start | bytes 2883584 | tf_op jit(solution)/shard_map/all_to_all | solution.py:110
  144.1 3.2 convert_element_type.70
  147.3 59.2 %all-to-all-done = bf16[8,64,1408]{2,1,0:T(8,128)(2,1)} async-done(((bf16[8,64,1408]{2,1,0:T(8,128)(2,1)}), bf16[8,64,1408]{2,1,0:T(8,128)(2,1)}, u32[]{:S(2)}, u32[]{:S(2)}) %all-to-all-start) | async-done | bytes 1441824 | tf_op jit(solution)/shard_map/all_to_all | solution.py:110
  209.9 38.1 %all_to_all.20 = bf16[8,64,1408]{2,1,0:T(8,128)(2,1)} all-to-all(bf16[8,64,1408]{2,1,0:T(8,128)(2,1)S(1)} %broadcast_in_dim.68), channel_id=1, replica_groups=mesh['blk'=32,'head'=8] {'head'}, dimensions={0} | all-to-all | bytes 2883584 | tf_op jit(solution)/shard_map/all_to_all | solution.py:40
  248.0 9.4 %convolution_convert_fusion = bf16[512,1408]{1,0:T(8,128)(2,1)} fusion(bf16[768,1408]{1,0:T(8,128)(2,1)S(1)} %copy-done, bf16[512,1408]{1,0:T(8,128)(2,1)} %bitcast.49, bf16[1408,768]{1,0:T(8,128)(2,1)} %param.19), kind=kOutput, calls=%fused_computation.11 | convolution fusion | flops 2240872448 | bytes 7208960 | tf_op jit(solution)/shard_map/dot_general | solution.py:118
  257.4 38.5 %all_to_all.21 = bf16[8,64,1408]{2,1,0:T(8,128)(2,1)S(1)} all-to-all(bf16[8,64,1408]{2,1,0:T(8,128)(2,1)} %bitcast.50), channel_id=1, replica_groups=mesh['blk'=32,'head'=8] {'head'}, dimensions={0} | all-to-all | bytes 2883584 | tf_op jit(solution)/shard_map/all_to_all | solution.py:119
  296.4 37.4 %all_to_all.22 = bf16[8,16,5632]{2,1,0:T(8,128)(2,1)S(1)} all-to-all(bf16[8,16,5632]{2,1,0:T(8,128)(2,1)S(1)} %broadcast_in_dim.70), channel_id=1, replica_groups=mesh['blk'=32,'head'=8] {'head'}, dimensions={0} | all-to-all | bytes 2883584 | tf_op jit(solution)/shard_map/all_to_all | solution.py:40
  333.8 3.6 abs_reduce_fusion
  339.4 3.4 collective-permute-done.9
  342.9 4.5 %collective-permute-done.10 = f32[48]{0:T(128)S(1)} collective-permute-done((f32[48]{0:T(128)S(1)}, f32[48]{0:T(128)S(1)}, u32[]{:S(2)}, u32[]{:S(2)}) %collective-permute-start.10) | collective-permute-done | bytes 224 | tf_op jit(solution)/shard_map/ppermute | solution.py:30
  347.5 5.3 %collective-permute-start.11 = (f32[48]{0:T(128)S(1)}, f32[48]{0:T(128)S(1)}, u32[]{:S(2)}, u32[]{:S(2)}) collective-permute-start(f32[48]{0:T(128)S(1)} %pad_maximum_fusion.4), channel_id=1, source_target_pairs={{0,8},{8,0},{16,24},{24,16},{32,40},{40,32},{48,56},{56,48},{64,72... | collective-permute-start | bytes 584 | tf_op jit(solution)/shard_map/ppermute | solution.py:30
  352.8 2.2 collective-permute-done.11
  356.7 2.1 collective-permute-done.12
  358.9 3.0 collective-permute-start.13
  362.0 2.0 collective-permute-done.13
  364.7 3.0 collective-permute-done.14
  367.9 2.1 collective-permute-start.15
  370.0 3.0 collective-permute-done.15
  (97 shorter events, 28.1 us)
Async XLA Ops:
  7.2 240.8 %copy-start = (bf16[768,1408]{1,0:T(8,128)(2,1)S(1)}, bf16[768,1408]{1,0:T(8,128)(2,1)}, u32[]{:S(2)}) copy-start(bf16[768,1408]{1,0:T(8,128)(2,1)} %param.20) | copy-start | bytes 6488068
  7.2 3.1 copy-start.7
  7.2 3.1 copy-start.8
  7.2 202.0 %all-gather.2.cloned.1.call-start = ((), (), s32[]{:S(2)}) async-start(), calls=%async_computation.4 | async-start | bytes 5947392 | tf_op jit(solution)/shard_map/all_gather | solution.py:108
  7.9 1.8 copy-start.1
  10.3 2.6 copy-start.5
  14.1 25.9 %collective-permute-start = (bf16[512,353]{0,1:T(8,128)(2,1)S(1)}, bf16[512,353]{0,1:T(8,128)(2,1)}, u32[]{:S(2)}, u32[]{:S(2)}) collective-permute-start(bf16[512,353]{0,1:T(8,128)(2,1)S(1)} %get-tuple-element.16), channel_id=1, source_target_pairs={{0,8},{8,16},{16,24},{24,32},{32,40},{40,48},{48,56},{56,64},{64,7... | collective-permute-start | bytes 1084424 | tf_op jit(solution)/shard_map/ppermute | solution.py:14
  23.2 27.4 %collective-permute-start.1 = (bf16[512,353]{0,1:T(8,128)(2,1)S(1)}, bf16[512,353]{0,1:T(8,128)(2,1)}, u32[]{:S(2)}, u32[]{:S(2)}) collective-permute-start(bf16[512,353]{0,1:T(8,128)(2,1)S(1)} %get-tuple-element.16), channel_id=1, source_target_pairs={{8,0},{16,8},{24,16},{32,24},{40,32},{48,40},{56,48},{64,56},{72,6... | collective-permute-start | bytes 1084424 | tf_op jit(solution)/shard_map/ppermute | solution.py:14
  27.5 26.7 %collective-permute-start.2 = (bf16[512,353]{0,1:T(8,128)(2,1)S(1)}, bf16[512,353]{0,1:T(8,128)(2,1)}, u32[]{:S(2)}, u32[]{:S(2)}) collective-permute-start(bf16[512,353]{0,1:T(8,128)(2,1)S(1)} %get-tuple-element.16), channel_id=1, source_target_pairs={{0,16},{8,24},{16,32},{24,40},{32,48},{40,56},{48,64},{56,72},{64,... | collective-permute-start | bytes 1084424 | tf_op jit(solution)/shard_map/ppermute | solution.py:14
  29.5 32.9 %collective-permute-start.3 = (bf16[512,353]{0,1:T(8,128)(2,1)S(1)}, bf16[512,353]{0,1:T(8,128)(2,1)S(1)}, u32[]{:S(2)}, u32[]{:S(2)}) collective-permute-start(bf16[512,353]{0,1:T(8,128)(2,1)S(1)} %get-tuple-element.16), channel_id=1, source_target_pairs={{16,0},{24,8},{32,16},{40,24},{48,32},{56,40},{64,48},{72,56},{80,... | collective-permute-start | bytes 1084424 | tf_op jit(solution)/shard_map/ppermute | solution.py:14
  35.5 27.7 %collective-permute-start.4 = (bf16[512,353]{0,1:T(8,128)(2,1)S(1)}, bf16[512,353]{0,1:T(8,128)(2,1)S(1)}, u32[]{:S(2)}, u32[]{:S(2)}) collective-permute-start(bf16[512,353]{0,1:T(8,128)(2,1)S(1)} %get-tuple-element.16), channel_id=1, source_target_pairs={{0,24},{8,32},{16,40},{24,48},{32,56},{40,64},{48,72},{56,80},{64,... | collective-permute-start | bytes 1084424 | tf_op jit(solution)/shard_map/ppermute | solution.py:14
  40.0 56.2 %collective-permute-start.5 = (bf16[512,353]{0,1:T(8,128)(2,1)S(1)}, bf16[512,353]{0,1:T(8,128)(2,1)S(1)}, u32[]{:S(2)}, u32[]{:S(2)}) collective-permute-start(bf16[512,353]{0,1:T(8,128)(2,1)S(1)} %get-tuple-element.16), channel_id=1, source_target_pairs={{24,0},{32,8},{40,16},{48,24},{56,32},{64,40},{72,48},{80,56},{88,... | collective-permute-start | bytes 1084424 | tf_op jit(solution)/shard_map/ppermute | solution.py:14
  50.6 46.4 %collective-permute-start.6 = (bf16[512,353]{0,1:T(8,128)(2,1)S(1)}, bf16[512,353]{0,1:T(8,128)(2,1)S(1)}, u32[]{:S(2)}, u32[]{:S(2)}) collective-permute-start(bf16[512,353]{0,1:T(8,128)(2,1)S(1)} %get-tuple-element.16), channel_id=1, source_target_pairs={{0,32},{8,40},{16,48},{24,56},{32,64},{40,72},{48,80},{56,88},{64,... | collective-permute-start | bytes 1084424 | tf_op jit(solution)/shard_map/ppermute | solution.py:14
  54.3 43.5 %collective-permute-start.7 = (bf16[512,353]{0,1:T(8,128)(2,1)S(1)}, bf16[512,353]{0,1:T(8,128)(2,1)S(1)}, u32[]{:S(2)}, u32[]{:S(2)}) collective-permute-start(bf16[512,353]{0,1:T(8,128)(2,1)S(1)} %get-tuple-element.16), channel_id=1, source_target_pairs={{32,0},{40,8},{48,16},{56,24},{64,32},{72,40},{80,48},{88,56},{96,... | collective-permute-start | bytes 1084424 | tf_op jit(solution)/shard_map/ppermute | solution.py:14
  129.5 3.0 copy-start.2
  134.2 72.3 %all-to-all-start = ((bf16[8,64,1408]{2,1,0:T(8,128)(2,1)}), bf16[8,64,1408]{2,1,0:T(8,128)(2,1)}, u32[]{:S(2)}, u32[]{:S(2)}) async-start(bf16[8,64,1408]{2,1,0:T(8,128)(2,1)} %bitcast.47), calls=%async_computation | async-start | bytes 2883584 | tf_op jit(solution)/shard_map/all_to_all | solution.py:110
  147.3 62.3 %copy-start.3 = (f32[1408]{0:T(1024)S(1)}, f32[1408]{0:T(1024)}, u32[]{:S(2)}) copy-start(f32[1408]{0:T(1024)} %param.18) | copy-start | bytes 16900
  147.3 62.3 %copy-start.4 = (f32[1408]{0:T(1024)S(1)}, f32[1408]{0:T(1024)}, u32[]{:S(2)}) copy-start(f32[1408]{0:T(1024)} %param.17) | copy-start | bytes 16900
  337.7 1.2 collective-permute-start.8
  339.1 3.6 collective-permute-start.9
  342.9 4.5 %collective-permute-start.10 = (f32[48]{0:T(128)S(1)}, f32[48]{0:T(128)S(1)}, u32[]{:S(2)}, u32[]{:S(2)}) collective-permute-start(f32[48]{0:T(128)S(1)} %pad_maximum_fusion.3), channel_id=1, source_target_pairs={{0,4},{1,5},{2,6},{3,7},{4,0},{5,1},{6,2},{7,3},{8,12},{9,13},{10,... | collective-permute-start | bytes 584 | tf_op jit(solution)/shard_map/ppermute | solution.py:30
  347.5 7.5 %collective-permute-start.11 = (f32[48]{0:T(128)S(1)}, f32[48]{0:T(128)S(1)}, u32[]{:S(2)}, u32[]{:S(2)}) collective-permute-start(f32[48]{0:T(128)S(1)} %pad_maximum_fusion.4), channel_id=1, source_target_pairs={{0,8},{8,0},{16,24},{24,16},{32,40},{40,32},{48,56},{56,48},{64,72... | collective-permute-start | bytes 584 | tf_op jit(solution)/shard_map/ppermute | solution.py:30
  355.2 3.6 collective-permute-start.12
  358.9 5.1 %collective-permute-start.13 = (f32[48]{0:T(128)S(1)}, f32[48]{0:T(128)S(1)}, u32[]{:S(2)}, u32[]{:S(2)}) collective-permute-start(f32[48]{0:T(128)S(1)} %pad_maximum_fusion.6), channel_id=1, source_target_pairs={{0,32},{8,40},{16,48},{24,56},{32,0},{40,8},{48,16},{56,24},{64,96... | collective-permute-start | bytes 584 | tf_op jit(solution)/shard_map/ppermute | solution.py:30
  364.2 3.6 collective-permute-start.14
  367.9 5.1 %collective-permute-start.15 = (f32[48]{0:T(128)S(1)}, f32[48]{0:T(128)S(1)}, u32[]{:S(2)}, u32[]{:S(2)}) collective-permute-start(f32[48]{0:T(128)S(1)} %pad_maximum_fusion.8), channel_id=1, source_target_pairs={{0,128},{8,136},{16,144},{24,152},{32,160},{40,168},{48,176},{56,1... | collective-permute-start | bytes 584 | tf_op jit(solution)/shard_map/ppermute | solution.py:30
  373.6 0.9 copy-start.6
Sparse Core Ops, SparseCore 0:
  11.4 172.8 all-gather.1
